TPU v7x, 32 devices: a whole 2x2x4 slice. The times are simulated.
32 devices in a mesh: freq: 16 (over z, y, core), rows: 2 (over x).
Axes of the slice: x: 2, y: 2, z: 4, core: 2. Of those that a mesh axis runs over, the one named last changes fastest.
Arguments:
- image_cube: float32 [2048, 64, 128], P('freq', 'rows'), may hold values from 0.05 to 2
- data_grad: float32 [2048, 64, 128], P('freq', 'rows'), may hold values from -4 to 4
- space_duals: float32 [4, 2048, 64, 128], P(None, 'freq', 'rows'), may hold values from -0.5 to 0.5
- freq_duals: float32 [8192, 2048], P(('rows', 'freq')), may hold values from -1 to 1
Outputs:
- image_next: float32 [2048, 64, 128], P('freq', 'rows')
- space_next: float32 [4, 2048, 64, 128], P(None, 'freq', 'rows')
- freq_next: float32 [8192, 2048], P(('rows', 'freq'))
All inputs are finite; a program needn't handle non-finite values.
Results may differ from a plain program's by a relative error of at most 0.00008.
Values sent between devices are 32-bit elements; how exact they have to be, the bound alone decides.
No kernel may reach another device: no remote copies, remote signals or barrier semaphores. Data moves between devices by JAX's collectives and lax.ppermute only.
A program may use at most 128 MiB of HBM per device.

v0:
```python
import math

import jax
import jax.numpy as jnp
from jax import lax
from jax.sharding import PartitionSpec as P

SCALES = 4


TAPS = (0.0625, 0.25, 0.375, 0.25, 0.0625)
SIGMA = 0.5
TAU_STEP = 0.5
SPACE_BOUND = 0.5
FREQ_BOUND = 1.0


def padded_2(cells, sides, width):
    for axis, dim in sides:
        count = lax.axis_size(axis)
        ends = count - 1
        head = lax.slice_in_dim(cells, 0, width, axis=dim)
        tail = lax.slice_in_dim(cells, cells.shape[dim] - width, cells.shape[dim], axis=dim)
        cells = jnp.concatenate(
            [
                lax.ppermute(tail, axis, [(i, (i + 1) % count) for i in range(ends)]),
                cells,
                lax.ppermute(head, axis, [((i + 1) % count, i) for i in range(ends)]),
            ],
            axis=dim,
        )
    return cells


def blur_rows(padded, dilation, out_rows):
    running = TAPS[0] * padded[:, 0:out_rows, :]
    for tap_idx in range(1, 5):
        offset = tap_idx * dilation
        running = running + TAPS[tap_idx] * padded[:, offset : offset + out_rows, :]
    return running


def blur_cols(planar, dilation):
    columns = planar.shape[2]
    reach_cols = 2 * dilation
    padded = jnp.pad(planar, ((0, 0), (0, 0), (reach_cols, reach_cols)))
    running = TAPS[0] * padded[:, :, 0:columns]
    for tap_idx in range(1, 5):
        offset = tap_idx * dilation
        running = running + TAPS[tap_idx] * padded[:, :, offset : offset + columns]
    return running


def inside_rows(margin, local_rows):
    first_row = lax.axis_index("rows") * local_rows - margin
    positions = first_row + jnp.arange(local_rows + 2 * margin, dtype=jnp.int32)
    limit = local_rows * lax.axis_size("rows")
    return ((positions >= 0) & (positions < limit)).astype(jnp.float32)[None, :, None]


def analyse(image_cube):
    local_rows = image_cube.shape[1]
    details = []
    depth = 2 ** (SCALES + 1) - 2
    current = padded_2(image_cube, (("rows", 1),), depth)
    inside = inside_rows(depth, local_rows)
    margin = depth
    for level_idx in range(SCALES):
        dilation = 2**level_idx
        reach_rows = 2 * dilation
        new_margin = margin - reach_rows
        out_rows = local_rows + 2 * new_margin
        start_row = depth - new_margin
        smoothed = blur_cols(blur_rows(current, dilation, out_rows), dilation)
        smoothed = smoothed * inside[:, start_row : start_row + out_rows, :]
        kept = current[:, reach_rows : reach_rows + out_rows, :] - smoothed
        details.append(kept[:, new_margin : new_margin + local_rows, :])
        current = smoothed
        margin = new_margin
    return details


def synthesise(space_next):
    local_rows = space_next.shape[2]
    running = jnp.zeros_like(space_next[0])
    for level_idx in reversed(range(SCALES)):
        dilation = 2**level_idx
        operand = running - space_next[level_idx]
        padded = padded_2(operand, (("rows", 1),), 2 * dilation)
        running = (
            blur_cols(blur_rows(padded, dilation, local_rows), dilation) + space_next[level_idx]
        )
    return running


def spectral(pixel_cube, freq_duals):
    chans_all, pixel_count = pixel_cube.shape
    block_size = min(512, chans_all)
    block_count = chans_all // block_size
    sample_idx = jnp.arange(chans_all, dtype=jnp.int32)
    highest = lax.Precision.HIGHEST

    def one_block(running, block_idx):
        first = block_idx * block_size
        coef_idx = first + jnp.arange(block_size, dtype=jnp.int32)
        phase = (2 * sample_idx[None, :] + 1) * coef_idx[:, None] % (4 * chans_all)
        weights = jnp.where(
            coef_idx == 0, math.sqrt(1.0 / chans_all), math.sqrt(2.0 / chans_all)
        ).astype(jnp.float32)
        table = jnp.cos(phase.astype(jnp.float32) * (math.pi / (2 * chans_all))) * weights[:, None]
        coeffs = lax.dot_general(
            pixel_cube,
            table,
            (((0,), (1,)), ((), ())),
            precision=highest,
            preferred_element_type=jnp.float32,
        )
        previous = lax.dynamic_slice_in_dim(freq_duals, first, block_size, 1)
        fresh = jnp.clip(previous + SIGMA * coeffs, -FREQ_BOUND, FREQ_BOUND)
        running = running + lax.dot_general(
            table,
            fresh,
            (((0,), (1,)), ((), ())),
            precision=highest,
            preferred_element_type=jnp.float32,
        )
        return (running, fresh)

    running, fresh_blocks = lax.scan(
        one_block,
        jnp.zeros((chans_all, pixel_count), jnp.float32),
        jnp.arange(block_count, dtype=jnp.int32),
    )
    freq_next = jnp.moveaxis(fresh_blocks, 0, 1).reshape(pixel_count, chans_all)
    return (running, freq_next)


def local(image_cube, data_grad, space_duals, freq_duals):
    chans, local_rows, columns = image_cube.shape
    peers = lax.axis_size("freq")
    share = local_rows * columns // peers
    pieces = image_cube.reshape(chans, peers, share)
    pixel_cube = lax.all_to_all(pieces, "freq", split_axis=1, concat_axis=0, tiled=True).reshape(
        chans * peers, share
    )
    details = analyse(image_cube)
    space_next = jnp.stack(
        [
            jnp.clip(space_duals[level_idx] + SIGMA * details[level_idx], -SPACE_BOUND, SPACE_BOUND)
            for level_idx in range(SCALES)
        ]
    )
    space_term = synthesise(space_next)
    spectral_sum, freq_next = spectral(pixel_cube, freq_duals)
    returned = lax.all_to_all(
        spectral_sum.reshape(chans * peers, 1, share),
        "freq",
        split_axis=0,
        concat_axis=1,
        tiled=True,
    )
    spectral_term = returned.reshape(chans, local_rows, columns)
    image_next = jnp.maximum(image_cube - TAU_STEP * (data_grad + space_term + spectral_term), 0.0)
    return (image_next, space_next, freq_next)


def solution(mesh):
    in_specs = (
        P("freq", "rows", None),
        P("freq", "rows", None),
        P(None, "freq", "rows", None),
        P(("rows", "freq"), None),
    )
    out_specs = (P("freq", "rows", None), P(None, "freq", "rows", None), P(("rows", "freq"), None))
    return jax.shard_map(local, mesh=mesh, in_specs=in_specs, out_specs=out_specs, check_vma=False)
```

profile of v0, /device:TPU:13, one launch (start us, length us, event | category | flops | bytes accessed | tf_op | source)
XLA Modules:
  0.0 414.0 jit_solution(241140880496741762)
XLA Ops:
  0.6 2.8 fusion.191
  3.4 2.4 copy.21
  5.9 4.5 %collective-permute-start = (f32[128,30,128]{2,0,1:T(8,128)}, f32[128,30,128]{2,0,1:T(8,128)}, u32[]{:S(2)}, u32[]{:S(2)}) collective-permute-start(f32[128,30,128]{2,0,1:T(8,128)} %copy.21), channel_id=1, source_target_pairs={{0,1},{2,3},{4,5},{6,7},{8,9},{10,11},{12,13},{14,15},{16,17},{18,... | collective-permute-start | bytes 5898248 | tf_op jit(solution)/shard_map/ppermute | solution.py:26
  10.4 2.4 copy.22
  14.1 1.6 reshape.59
  15.7 4.1 copy.15
  19.8 7.2 %all-to-all-start = ((f32[128,16,256]{2,0,1:T(8,128)}), f32[128,16,256]{2,0,1:T(8,128)}, u32[]{:S(2)}, u32[]{:S(2)}) async-start(f32[128,16,256]{2,0,1:T(8,128)} %copy.15), calls=%async_computation | async-start | bytes 4194304 | tf_op jit(solution)/shard_map/all_to_all | solution.py:143
  27.3 23.5 %collective-permute-done = f32[128,30,128]{2,0,1:T(8,128)} collective-permute-done((f32[128,30,128]{2,0,1:T(8,128)}, f32[128,30,128]{2,0,1:T(8,128)}, u32[]{:S(2)}, u32[]{:S(2)}) %collective-permute-start) | collective-permute-done | bytes 1966112 | tf_op jit(solution)/shard_map/ppermute | solution.py:26
  50.9 2.7 copy.13
  53.6 4.8 %collective-permute-done.1 = f32[128,30,128]{2,0,1:T(8,128)} collective-permute-done((f32[128,30,128]{2,0,1:T(8,128)}, f32[128,30,128]{2,0,1:T(8,128)}, u32[]{:S(2)}, u32[]{:S(2)}) %collective-permute-start.1) | collective-permute-done | bytes 1966112 | tf_op jit(solution)/shard_map/ppermute | solution.py:28
  58.3 2.7 copy.14
  61.8 4.8 %fusion.184 = (f32[128,88,128]{2,1,0:T(8,128)}, f32[128,88,128]{2,1,0:T(8,128)S(1)}) fusion(f32[128,92,128]{2,1,0:T(8,128)S(1)} %pad_maximum_fusion.1), kind=kLoop, calls=%fused_computation.263 | loop fusion | flops 12976128 | bytes 40370176 | tf_op jit(solution)/shard_map/slice | solution.py:39
  66.6 6.1 %fusion.36 = f32[128,88,128]{2,1,0:T(8,128)S(1)} fusion(f32[128,88,128]{2,1,0:T(8,128)S(1)} %get-tuple-element.154, f32[88]{0:T(128)S(1)} %slice_bitcast_fusion.3), kind=kLoop, calls=%fused_computation.70 | loop fusion | flops 14417920 | bytes 11534688 | tf_op jit(solution)/shard_map/mul | solution.py:75
  72.7 4.2 %fusion.185 = (f32[128,80,128]{2,1,0:T(8,128)}, f32[128,80,128]{2,1,0:T(8,128)S(1)}) fusion(f32[128,88,128]{2,1,0:T(8,128)S(1)} %fusion.36), kind=kLoop, calls=%fused_computation.264 | loop fusion | flops 11796480 | bytes 36700160 | tf_op jit(solution)/shard_map/slice | solution.py:39
  76.9 5.6 %fusion.49 = f32[128,80,128]{2,1,0:T(8,128)S(1)} fusion(f32[128,80,128]{2,1,0:T(8,128)S(1)} %get-tuple-element.156, f32[80]{0:T(128)S(1)} %slice_bitcast_fusion.2), kind=kLoop, calls=%fused_computation.87 | loop fusion | flops 13107200 | bytes 10486080 | tf_op jit(solution)/shard_map/mul | solution.py:75
  82.5 4.2 %fusion.186 = (f32[128,64,128]{2,1,0:T(8,128)}, f32[128,64,128]{2,1,0:T(8,128)S(1)}) fusion(f32[128,80,128]{2,1,0:T(8,128)S(1)} %fusion.49), kind=kLoop, calls=%fused_computation.265 | loop fusion | flops 9437184 | bytes 29360128 | tf_op jit(solution)/shard_map/slice | solution.py:39
  86.7 4.5 %fusion.62 = f32[128,64,128]{2,1,0:T(8,128)S(1)} fusion(f32[128,64,128]{2,1,0:T(8,128)S(1)} %get-tuple-element.158, f32[64]{0:T(128)S(1)} %slice_bitcast_fusion.1), kind=kLoop, calls=%fused_computation.104 | loop fusion | flops 10485760 | bytes 8388864 | tf_op jit(solution)/shard_map/mul | solution.py:75
  93.2 4.6 %broadcast_subtract_fusion = (f32[128,32,128]{2,1,0:T(8,128)S(1)}, f32[128,32,128]{2,1,0:T(8,128)}) fusion(f32[32]{0:T(128)S(1)} %slice_bitcast_fusion, f32[128,32,128]{2,1,0:T(8,128)S(1)} %fusion.176, f32[128,64,128]{2,1,0:T(8,128)S(1)} %fusion.62, f32[4,128,32,128]{3,2,1,0:T(8,128)} %param.8), kind=kLoop, calls=%fused_computation.257 | loop fusion | flops 7864320 | bytes 10485888 | tf_op jit(solution)/shard_map/sub | solution.py:88
  99.1 1.5 fusion.190
  103.3 19.6 %collective-permute-done.2 = f32[128,16,128]{2,1,0:T(8,128)S(1)} collective-permute-done((f32[128,16,128]{2,1,0:T(8,128)}, f32[128,16,128]{2,1,0:T(8,128)S(1)}, u32[]{:S(2)}, u32[]{:S(2)}) %collective-permute-start.2) | collective-permute-done | bytes 1048608 | tf_op jit(solution)/shard_map/ppermute | solution.py:26
  122.9 3.9 collective-permute-done.3
  126.8 4.4 %fusion.97 = f32[128,32,128]{2,1,0:T(8,128)S(1)} fusion(f32[128,32,128]{2,1,0:T(8,128)} %copy-done.5, f32[128,16,128]{2,1,0:T(8,128)} %collective-permute-done.3, f32[128,16,128]{2,1,0:T(8,128)S(1)} %collective-permute-done.2), kind=kLoop, calls=%fused_computation.159 | loop fusion | flops 6815744 | bytes 6291456 | tf_op jit(solution)/shard_map/add | solution.py:39
  131.2 4.8 %fusion.121 = (f32[128,32,128]{2,1,0:T(8,128)S(1)}, f32[128,32,128]{2,1,0:T(8,128)}) fusion(f32[128,32,128]{2,1,0:T(8,128)S(1)} %copy-done.7, f32[128,32,128]{2,1,0:T(8,128)S(1)} %fusion.97, f32[128,64,128]{2,1,0:T(8,128)S(1)} %copy-done.3, f32[128,64,128]{2,1,0:T(8,128)} %get-tuple-element.157, f32[4,128,32,128]{3,2,1,0:T(8,128)} %param.8), kind=kLoop, calls=%fused_computation.183 | loop fusion | flops 7864320 | bytes 14680064 | tf_op jit(solution)/shard_map/sub | solution.py:88
  138.4 2.1 collective-permute-start.4
  141.8 193.9 %while.15 = (s32[]{:T(128)}, f32[2048,256]{1,0:T(8,128)}, f32[4,256,512]{1,2,0:T(8,128)}, s32[4]{0:T(128)S(1)}, f32[256,2048]{1,0:T(8,128)}, /*index=5*/f32[2048...) while((s32[]{:T(128)}, f32[2048,256]{1,0:T(8,128)}, f32[4,256,512]{1,2,0:T(8,128)}, ...), condition=%wide.region_1.2_spmd.clone, body=%wide.region_0.1_spmd.clone.sunk | while | flops 6475356160 | bytes 10523317 | solution.py:129
  144.4 21.8 %bitcast_dynamic-update-slice_fusion.2 = (f32[4,256,512]{1,2,0:T(8,128)}, f32[256,512]{0,1:T(8,128)}) fusion(f32[4,256,512]{1,2,0:T(8,128)} %get-tuple-element.222, s32[]{:T(128)} %get-tuple-element.220, f32[256,512]{0,1:T(8,128)S(1)} %copy.24, f32[2048,256]{1,0:T(8,128)} %get-tuple-element.235, f32[512]{0:T(512)S(1)} %compare_select_fusion.2, ...), kind=kOutput, calls=%fused_computation.17.clone.1 | convolution fusion | flops 3237347328 | bytes 3682816 | tf_op jit(solution)/shard_map/while/body/eval_jaxpr/dot_general | solution.py:111
  166.2 23.9 %convolution_add_fusion.2 = f32[2048,256]{1,0:T(8,128)} fusion(f32[256,512]{0,1:T(8,128)} %get-tuple-element.208, f32[2048,256]{1,0:T(8,128)} %get-tuple-element.221, f32[512]{0:T(512)S(1)} %compare_select_fusion.2, s32[512]{0:T(512)S(1)} %iota_add_fusion.2, s32[2048]{0:T(1024)S(1)} %fusion.201, pred[]{:T(512)S(6)} %compare.12), kind=kOutput, calls=%fused_computation.11.clone.1 | convolution fusion | flops 3238002688 | bytes 4730881 | tf_op jit(solution)/shard_map/while/body/eval_jaxpr/dot_general | solution.py:120
  192.6 21.8 %bitcast_dynamic-update-slice_fusion.2 = (f32[4,256,512]{1,2,0:T(8,128)}, f32[256,512]{0,1:T(8,128)}) fusion(f32[4,256,512]{1,2,0:T(8,128)} %get-tuple-element.222, s32[]{:T(128)} %get-tuple-element.220, f32[256,512]{0,1:T(8,128)S(1)} %copy.24, f32[2048,256]{1,0:T(8,128)} %get-tuple-element.235, f32[512]{0:T(512)S(1)} %compare_select_fusion.2, ...), kind=kOutput, calls=%fused_computation.17.clone.1 | convolution fusion | flops 3237347328 | bytes 3682816 | tf_op jit(solution)/shard_map/while/body/eval_jaxpr/dot_general | solution.py:111
  214.3 24.2 %convolution_add_fusion.2 = f32[2048,256]{1,0:T(8,128)} fusion(f32[256,512]{0,1:T(8,128)} %get-tuple-element.208, f32[2048,256]{1,0:T(8,128)} %get-tuple-element.221, f32[512]{0:T(512)S(1)} %compare_select_fusion.2, s32[512]{0:T(512)S(1)} %iota_add_fusion.2, s32[2048]{0:T(1024)S(1)} %fusion.201, pred[]{:T(512)S(6)} %compare.12), kind=kOutput, calls=%fused_computation.11.clone.1 | convolution fusion | flops 3238002688 | bytes 4730881 | tf_op jit(solution)/shard_map/while/body/eval_jaxpr/dot_general | solution.py:120
  241.0 21.8 %bitcast_dynamic-update-slice_fusion.2 = (f32[4,256,512]{1,2,0:T(8,128)}, f32[256,512]{0,1:T(8,128)}) fusion(f32[4,256,512]{1,2,0:T(8,128)} %get-tuple-element.222, s32[]{:T(128)} %get-tuple-element.220, f32[256,512]{0,1:T(8,128)S(1)} %copy.24, f32[2048,256]{1,0:T(8,128)} %get-tuple-element.235, f32[512]{0:T(512)S(1)} %compare_select_fusion.2, ...), kind=kOutput, calls=%fused_computation.17.clone.1 | convolution fusion | flops 3237347328 | bytes 3682816 | tf_op jit(solution)/shard_map/while/body/eval_jaxpr/dot_general | solution.py:111
  262.8 24.2 %convolution_add_fusion.2 = f32[2048,256]{1,0:T(8,128)} fusion(f32[256,512]{0,1:T(8,128)} %get-tuple-element.208, f32[2048,256]{1,0:T(8,128)} %get-tuple-element.221, f32[512]{0:T(512)S(1)} %compare_select_fusion.2, s32[512]{0:T(512)S(1)} %iota_add_fusion.2, s32[2048]{0:T(1024)S(1)} %fusion.201, pred[]{:T(512)S(6)} %compare.12), kind=kOutput, calls=%fused_computation.11.clone.1 | convolution fusion | flops 3238002688 | bytes 4730881 | tf_op jit(solution)/shard_map/while/body/eval_jaxpr/dot_general | solution.py:120
  289.5 21.8 %bitcast_dynamic-update-slice_fusion.2 = (f32[4,256,512]{1,2,0:T(8,128)}, f32[256,512]{0,1:T(8,128)}) fusion(f32[4,256,512]{1,2,0:T(8,128)} %get-tuple-element.222, s32[]{:T(128)} %get-tuple-element.220, f32[256,512]{0,1:T(8,128)S(1)} %copy.24, f32[2048,256]{1,0:T(8,128)} %get-tuple-element.235, f32[512]{0:T(512)S(1)} %compare_select_fusion.2, ...), kind=kOutput, calls=%fused_computation.17.clone.1 | convolution fusion | flops 3237347328 | bytes 3682816 | tf_op jit(solution)/shard_map/while/body/eval_jaxpr/dot_general | solution.py:111
  311.3 24.2 %convolution_add_fusion.2 = f32[2048,256]{1,0:T(8,128)} fusion(f32[256,512]{0,1:T(8,128)} %get-tuple-element.208, f32[2048,256]{1,0:T(8,128)} %get-tuple-element.221, f32[512]{0:T(512)S(1)} %compare_select_fusion.2, s32[512]{0:T(512)S(1)} %iota_add_fusion.2, s32[2048]{0:T(1024)S(1)} %fusion.201, pred[]{:T(512)S(6)} %compare.12), kind=kOutput, calls=%fused_computation.11.clone.1 | convolution fusion | flops 3238002688 | bytes 4730881 | tf_op jit(solution)/shard_map/while/body/eval_jaxpr/dot_general | solution.py:120
  335.7 4.4 %reshape.61 = f32[2048,1,256]{2,1,0:T(1,128)} reshape(f32[2048,256]{1,0:T(8,128)} %get-tuple-element.94) | data formatting | bytes 4194304 | tf_op jit(solution)/shard_map/reshape | solution.py:156
  340.1 9.0 %all-to-all-start.1 = ((f32[2048,1,256]{2,1,0:T(1,128)}), f32[2048,1,256]{2,1,0:T(1,128)}, u32[]{:S(2)}, u32[]{:S(2)}) async-start(f32[2048,1,256]{2,1,0:T(1,128)} %reshape.61), calls=%async_computation.1 | async-start | bytes 4194304 | tf_op jit(solution)/shard_map/all_to_all | solution.py:155
  349.1 6.3 %fusion.89 = f32[128,32,128]{2,1,0:T(8,128)S(1)} fusion(f32[128,32,128]{2,1,0:T(8,128)} %copy-done.10, f32[128,8,128]{2,1,0:T(8,128)} %collective-permute-done.5, f32[128,8,128]{2,1,0:T(8,128)} %collective-permute-done.4), kind=kLoop, calls=%fused_computation.151 | loop fusion | flops 6815744 | bytes 5242880 | tf_op jit(solution)/shard_map/add | solution.py:39
  355.4 4.2 %fusion.131 = (f32[128,32,128]{2,1,0:T(8,128)S(1)}, f32[128,32,128]{2,1,0:T(8,128)S(1)}) fusion(f32[128,32,128]{2,1,0:T(8,128)S(1)} %copy-done.6, f32[128,32,128]{2,1,0:T(8,128)S(1)} %fusion.89, f32[128,80,128]{2,1,0:T(8,128)} %copy-done.1, f32[128,80,128]{2,1,0:T(8,128)} %get-tuple-element.155, f32[4,128,32,128]{3,2,1,0:T(8,128)} %param.8), kind=kLoop, calls=%fused_computation.193 | loop fusion | flops 7864320 | bytes 14680064 | tf_op jit(solution)/shard_map/sub | solution.py:88
  359.7 5.0 %collective-permute-start.6 = (f32[128,4,128]{2,1,0:T(4,128)S(1)}, f32[128,4,128]{2,1,0:T(4,128)S(1)}, u32[]{:S(2)}, u32[]{:S(2)}) collective-permute-start(f32[128,4,128]{2,1,0:T(4,128)S(1)} %get-tuple-element.161), channel_id=1, source_target_pairs={{0,1},{2,3},{4,5},{6,7},{8,9},{10,11},{12,13},{14,15},{16,17},{18,... | collective-permute-start | bytes 786440 | tf_op jit(solution)/shard_map/ppermute | solution.py:26
  366.1 4.0 collective-permute-done.6
  370.1 3.8 collective-permute-done.7
  373.9 1.6 fusion.81
  375.5 4.6 %fusion.141 = (f32[128,32,128]{2,1,0:T(8,128)S(1)}, f32[128,32,128]{2,1,0:T(8,128)S(1)}) fusion(f32[128,32,128]{2,1,0:T(8,128)S(1)} %get-tuple-element.146, f32[128,32,128]{2,1,0:T(8,128)S(1)} %fusion.81, f32[128,88,128]{2,1,0:T(8,128)} %copy-done, f32[128,88,128]{2,1,0:T(8,128)} %get-tuple-element.153, f32[4,128,32,128]{3,2,1,0:T(8,128)} %param.8), kind=kLoop, calls=%fused_computation.203 | loop fusion | flops 7864320 | bytes 14680064 | tf_op jit(solution)/shard_map/sub | solution.py:88
  382.8 3.9 pad_maximum_fusion
  386.7 2.9 copy.19
  389.5 7.4 %fusion.73 = f32[128,32,128]{2,1,0:T(8,128)} fusion(f32[128,32,128]{2,1,0:T(8,128)} %copy-done.11, f32[128,2,128]{2,1,0:T(2,128)S(1)} %collective-permute-done.9, f32[128,2,128]{2,1,0:T(2,128)S(1)} %collective-permute-done.8), kind=kLoop, calls=%fused_computation.135 | loop fusion | flops 6815744 | bytes 4456448 | tf_op jit(solution)/shard_map/add | solution.py:39
  396.9 4.1 copy.17
  401.1 2.6 reshape.62
  403.7 9.9 %fusion.155 = f32[128,32,128]{2,1,0:T(8,128)} fusion(f32[128,32,128]{2,1,0:T(8,128)S(1)} %copy-done.4, f32[128,32,128]{2,1,0:T(8,128)} %reshape.62, f32[128,32,128]{2,1,0:T(8,128)} %param.7, f32[128,32,128]{2,1,0:T(8,128)} %copy-done.9, f32[128,32,128]{2,1,0:T(8,128)} %fusion.73), kind=kLoop, calls=%fused_computation.217 | loop fusion | flops 7864320 | bytes 12582912 | tf_op jit(solution)/shard_map/max | solution.py:163
  (74 shorter events, 23.4 us)
Async XLA Ops:
  5.9 8.2 %copy-start.4 = (f32[128,32,128]{2,1,0:T(8,128)S(1)}, f32[128,32,128]{2,1,0:T(8,128)}, u32[]{:S(2)}) copy-start(f32[128,32,128]{2,1,0:T(8,128)} %param.6) | copy-start | bytes 6291460
  5.9 45.0 %collective-permute-start = (f32[128,30,128]{2,0,1:T(8,128)}, f32[128,30,128]{2,0,1:T(8,128)}, u32[]{:S(2)}, u32[]{:S(2)}) collective-permute-start(f32[128,30,128]{2,0,1:T(8,128)} %copy.21), channel_id=1, source_target_pairs={{0,1},{2,3},{4,5},{6,7},{8,9},{10,11},{12,13},{14,15},{16,17},{18,... | collective-permute-start | bytes 5898248 | tf_op jit(solution)/shard_map/ppermute | solution.py:26
  12.8 45.6 %collective-permute-start.1 = (f32[128,30,128]{2,0,1:T(8,128)}, f32[128,30,128]{2,0,1:T(8,128)}, u32[]{:S(2)}, u32[]{:S(2)}) collective-permute-start(f32[128,30,128]{2,0,1:T(8,128)} %copy.22), channel_id=1, source_target_pairs={{1,0},{3,2},{5,4},{7,6},{9,8},{11,10},{13,12},{15,14},{17,16},{19,... | collective-permute-start | bytes 5898248 | tf_op jit(solution)/shard_map/ppermute | solution.py:28
  19.8 121.9 %all-to-all-start = ((f32[128,16,256]{2,0,1:T(8,128)}), f32[128,16,256]{2,0,1:T(8,128)}, u32[]{:S(2)}, u32[]{:S(2)}) async-start(f32[128,16,256]{2,0,1:T(8,128)} %copy.15), calls=%async_computation | async-start | bytes 4194304 | tf_op jit(solution)/shard_map/all_to_all | solution.py:143
  72.7 4.2 %copy-start = (f32[128,88,128]{2,1,0:T(8,128)}, f32[128,88,128]{2,1,0:T(8,128)S(1)}, u32[]{:S(2)}) copy-start(f32[128,88,128]{2,1,0:T(8,128)S(1)} %fusion.36) | copy-start | bytes 17301508
  82.5 4.2 %copy-start.1 = (f32[128,80,128]{2,1,0:T(8,128)}, f32[128,80,128]{2,1,0:T(8,128)S(1)}, u32[]{:S(2)}) copy-start(f32[128,80,128]{2,1,0:T(8,128)S(1)} %fusion.49) | copy-start | bytes 15728644
  91.2 2.0 copy-start.2
  97.8 1.3 copy-start.5
  100.6 22.3 %collective-permute-start.2 = (f32[128,16,128]{2,1,0:T(8,128)}, f32[128,16,128]{2,1,0:T(8,128)S(1)}, u32[]{:S(2)}, u32[]{:S(2)}) collective-permute-start(f32[128,16,128]{2,1,0:T(8,128)} %get-tuple-element.165), channel_id=1, source_target_pairs={{0,1},{2,3},{4,5},{6,7},{8,9},{10,11},{12,13},{14,15},{16,17},{18,... | collective-permute-start | bytes 3145736 | tf_op jit(solution)/shard_map/ppermute | solution.py:26
  101.9 24.8 %collective-permute-start.3 = (f32[128,16,128]{2,1,0:T(8,128)}, f32[128,16,128]{2,1,0:T(8,128)}, u32[]{:S(2)}, u32[]{:S(2)}) collective-permute-start(f32[128,16,128]{2,1,0:T(8,128)} %get-tuple-element.166), channel_id=1, source_target_pairs={{1,0},{3,2},{5,4},{7,6},{9,8},{11,10},{13,12},{15,14},{17,16},{19,... | collective-permute-start | bytes 3145736 | tf_op jit(solution)/shard_map/ppermute | solution.py:28
  103.2 27.9 %copy-start.3 = (f32[128,64,128]{2,1,0:T(8,128)S(1)}, f32[128,64,128]{2,1,0:T(8,128)}, u32[]{:S(2)}) copy-start(f32[128,64,128]{2,1,0:T(8,128)} %copy-done.2) | copy-start | bytes 12582916
  103.2 27.9 %copy-start.7 = (f32[128,32,128]{2,1,0:T(8,128)S(1)}, f32[128,32,128]{2,1,0:T(8,128)}, u32[]{:S(2)}) copy-start(f32[128,32,128]{2,1,0:T(8,128)} %get-tuple-element.150) | copy-start | bytes 6291460
  136.0 1.4 copy-start.10
  138.4 210.7 %collective-permute-start.4 = (f32[128,8,128]{2,1,0:T(8,128)}, f32[128,8,128]{2,1,0:T(8,128)}, u32[]{:S(2)}, u32[]{:S(2)}) collective-permute-start(f32[128,8,128]{2,1,0:T(8,128)} %get-tuple-element.163), channel_id=1, source_target_pairs={{0,1},{2,3},{4,5},{6,7},{8,9},{10,11},{12,13},{14,15},{16,17},{18,... | collective-permute-start | bytes 1572872 | tf_op jit(solution)/shard_map/ppermute | solution.py:26
  140.5 208.7 %collective-permute-start.5 = (f32[128,8,128]{2,1,0:T(8,128)}, f32[128,8,128]{2,1,0:T(8,128)}, u32[]{:S(2)}, u32[]{:S(2)}) collective-permute-start(f32[128,8,128]{2,1,0:T(8,128)} %get-tuple-element.164), channel_id=1, source_target_pairs={{1,0},{3,2},{5,4},{7,6},{9,8},{11,10},{13,12},{15,14},{17,16},{19,... | collective-permute-start | bytes 1572872 | tf_op jit(solution)/shard_map/ppermute | solution.py:28
  340.1 56.8 %all-to-all-start.1 = ((f32[2048,1,256]{2,1,0:T(1,128)}), f32[2048,1,256]{2,1,0:T(1,128)}, u32[]{:S(2)}, u32[]{:S(2)}) async-start(f32[2048,1,256]{2,1,0:T(1,128)} %reshape.61), calls=%async_computation.1 | async-start | bytes 4194304 | tf_op jit(solution)/shard_map/all_to_all | solution.py:155
  349.1 6.3 %copy-start.6 = (f32[128,32,128]{2,1,0:T(8,128)S(1)}, f32[128,32,128]{2,1,0:T(8,128)}, u32[]{:S(2)}) copy-start(f32[128,32,128]{2,1,0:T(8,128)} %get-tuple-element.148) | copy-start | bytes 6291460
  359.7 10.3 %collective-permute-start.6 = (f32[128,4,128]{2,1,0:T(4,128)S(1)}, f32[128,4,128]{2,1,0:T(4,128)S(1)}, u32[]{:S(2)}, u32[]{:S(2)}) collective-permute-start(f32[128,4,128]{2,1,0:T(4,128)S(1)} %get-tuple-element.161), channel_id=1, source_target_pairs={{0,1},{2,3},{4,5},{6,7},{8,9},{10,11},{12,13},{14,15},{16,17},{18,... | collective-permute-start | bytes 786440 | tf_op jit(solution)/shard_map/ppermute | solution.py:26
  364.8 9.1 %collective-permute-start.7 = (f32[128,4,128]{2,1,0:T(4,128)S(1)}, f32[128,4,128]{2,1,0:T(4,128)S(1)}, u32[]{:S(2)}, u32[]{:S(2)}) collective-permute-start(f32[128,4,128]{2,1,0:T(4,128)S(1)} %get-tuple-element.162), channel_id=1, source_target_pairs={{1,0},{3,2},{5,4},{7,6},{9,8},{11,10},{13,12},{15,14},{17,16},{19,... | collective-permute-start | bytes 786440 | tf_op jit(solution)/shard_map/ppermute | solution.py:28
  375.5 7.3 %copy-start.8 = (f32[128,32,128]{2,1,0:T(8,128)S(1)}, f32[128,32,128]{2,1,0:T(8,128)}, u32[]{:S(2)}) copy-start(f32[128,32,128]{2,1,0:T(8,128)} %get-tuple-element.150) | copy-start | bytes 6291460
  380.1 6.6 %copy-start.9 = (f32[128,32,128]{2,1,0:T(8,128)}, f32[128,32,128]{2,1,0:T(8,128)S(1)}, u32[]{:S(2)}) copy-start(f32[128,32,128]{2,1,0:T(8,128)S(1)} %get-tuple-element.144) | copy-start | bytes 6291460
  380.1 6.6 %copy-start.11 = (f32[128,32,128]{2,1,0:T(8,128)}, f32[128,32,128]{2,1,0:T(8,128)S(1)}, u32[]{:S(2)}) copy-start(f32[128,32,128]{2,1,0:T(8,128)S(1)} %get-tuple-element.143) | copy-start | bytes 6291460
  380.2 9.4 %collective-permute-start.8 = (f32[128,2,128]{2,1,0:T(2,128)S(1)}, f32[128,2,128]{2,1,0:T(2,128)S(1)}, u32[]{:S(2)}, u32[]{:S(2)}) collective-permute-start(f32[128,2,128]{2,1,0:T(2,128)S(1)} %get-tuple-element.159), channel_id=1, source_target_pairs={{0,1},{2,3},{4,5},{6,7},{8,9},{10,11},{12,13},{14,15},{16,17},{18,... | collective-permute-start | bytes 393224 | tf_op jit(solution)/shard_map/ppermute | solution.py:26
  381.5 8.1 %collective-permute-start.9 = (f32[128,2,128]{2,1,0:T(2,128)S(1)}, f32[128,2,128]{2,1,0:T(2,128)S(1)}, u32[]{:S(2)}, u32[]{:S(2)}) collective-permute-start(f32[128,2,128]{2,1,0:T(2,128)S(1)} %get-tuple-element.160), channel_id=1, source_target_pairs={{1,0},{3,2},{5,4},{7,6},{9,8},{11,10},{13,12},{15,14},{17,16},{19,... | collective-permute-start | bytes 393224 | tf_op jit(solution)/shard_map/ppermute | solution.py:28
where the time goes:
time: 422 us; the launch traced here: 414 us
  matrix products  184 us (44%)
  other arithmetic  82.4 us (20%)
  waiting for transfers between devices  59.6 us (14%)
  local copies, waits for them, and re-layouts  47.2 us (11%)
  starting transfers between devices  36.9 us (9%)
    dot_general x4, matrix products, one_block(): lax.dot_general(table, fresh, (((0,), (1,)), ((), ())), precision=highest...  96.7 us
    dot_general x4, matrix products, one_block(): lax.dot_general(pixel_cube, table, (((0,), (1,)), ((), ())), precision=hi...  87.1 us
    ppermute x5, waiting for transfers between devices, padded_2(): lax.ppermute(tail, axis, [(i, (i + 1) % count) for i in range(ends)])  47.1 us
    add x5, other arithmetic, blur_rows(): running = running + TAPS[tap_idx] * padded[:, offset:offset + out_rows, :]  20.2 us
    sub x4, other arithmetic, synthesise(): operand = running - space_next[level_idx]  18.2 us
    mul x3, other arithmetic, analyse(): smoothed = smoothed * inside[:, start_row:start_row + out_rows, :]  16.2 us
    ppermute x5, starting transfers between devices, padded_2(): lax.ppermute(tail, axis, [(i, (i + 1) % count) for i in range(ends)])  14.3 us
    slice x3, other arithmetic, blur_rows(): running = running + TAPS[tap_idx] * padded[:, offset:offset + out_rows, :]  13.2 us
  transfers between devices with their start and end apart: 12, of which 6 were waited for; matrix products, arithmetic and copies ran while one was open for 69% of the time, Pallas kernels for 0%

commit v1 on v0

--- a/solution.py
+++ b/solution.py
@@ -93,45 +93,45 @@
     return running
 
 
+def dct_table(length):
+    split = 64 if length % 64 == 0 else 1
+    groups = length // split
+    period = 4 * length
+    coef_idx = jnp.arange(length, dtype=jnp.int32)
+    scale = math.pi / (2 * length)
+    outer_phase = (coef_idx[:, None] * (2 * split * jnp.arange(groups, dtype=jnp.int32))[None, :]) % period
+    inner_phase = (coef_idx[:, None] * (2 * jnp.arange(split, dtype=jnp.int32) + 1)[None, :]) % period
+    outer_angle = outer_phase.astype(jnp.float32) * scale
+    inner_angle = inner_phase.astype(jnp.float32) * scale
+    weights = jnp.where(
+        coef_idx == 0, math.sqrt(1.0 / length), math.sqrt(2.0 / length)
+    ).astype(jnp.float32)[:, None, None]
+    table = (
+        jnp.cos(outer_angle)[:, :, None] * jnp.cos(inner_angle)[:, None, :]
+        - jnp.sin(outer_angle)[:, :, None] * jnp.sin(inner_angle)[:, None, :]
+    ) * weights
+    return table.reshape(length, length)
+
+
 def spectral(pixel_cube, freq_duals):
     chans_all, pixel_count = pixel_cube.shape
-    block_size = min(512, chans_all)
-    block_count = chans_all // block_size
-    sample_idx = jnp.arange(chans_all, dtype=jnp.int32)
-    highest = lax.Precision.HIGHEST
-
-    def one_block(running, block_idx):
-        first = block_idx * block_size
-        coef_idx = first + jnp.arange(block_size, dtype=jnp.int32)
-        phase = (2 * sample_idx[None, :] + 1) * coef_idx[:, None] % (4 * chans_all)
-        weights = jnp.where(
-            coef_idx == 0, math.sqrt(1.0 / chans_all), math.sqrt(2.0 / chans_all)
-        ).astype(jnp.float32)
-        table = jnp.cos(phase.astype(jnp.float32) * (math.pi / (2 * chans_all))) * weights[:, None]
-        coeffs = lax.dot_general(
-            pixel_cube,
-            table,
-            (((0,), (1,)), ((), ())),
-            precision=highest,
-            preferred_element_type=jnp.float32,
-        )
-        previous = lax.dynamic_slice_in_dim(freq_duals, first, block_size, 1)
-        fresh = jnp.clip(previous + SIGMA * coeffs, -FREQ_BOUND, FREQ_BOUND)
-        running = running + lax.dot_general(
-            table,
-            fresh,
-            (((0,), (1,)), ((), ())),
-            precision=highest,
-            preferred_element_type=jnp.float32,
-        )
-        return (running, fresh)
-
-    running, fresh_blocks = lax.scan(
-        one_block,
-        jnp.zeros((chans_all, pixel_count), jnp.float32),
-        jnp.arange(block_count, dtype=jnp.int32),
+    precision = lax.Precision.HIGH
+    table = dct_table(chans_all)
+    coeffs = lax.dot_general(
+        pixel_cube,
+        table,
+        (((0,), (1,)), ((), ())),
+        precision=precision,
+        preferred_element_type=jnp.float32,
     )
-    freq_next = jnp.moveaxis(fresh_blocks, 0, 1).reshape(pixel_count, chans_all)
+    freq_next = jnp.clip(freq_duals + SIGMA * coeffs, -FREQ_BOUND, FREQ_BOUND)
+    running = lax.dot_general(
+        table,
+        freq_next,
+        (((0,), (1,)), ((), ())),
+        precision=precision,
+        preferred_element_type=jnp.float32,
+    )
     return (running, freq_next)
 
 

time: 422 us -> 262 us (0.62)
  the two profiles are of different devices: /device:TPU:13 before, /device:TPU:0 now
where the time goes in v1:
time: 262 us; the launch traced here: 257 us
  other arithmetic  97.7 us (37%)
  starting transfers between devices  45.3 us (17%)
  local copies, waits for them, and re-layouts  44.3 us (17%)
  waiting for transfers between devices  39.7 us (15%)
  matrix products  28.7 us (11%)
    ppermute x5, waiting for transfers between devices, padded_2(): lax.ppermute(head, axis, [((i + 1) % count, i) for i in range(ends)])  35 us
    ppermute x5, starting transfers between devices, padded_2(): lax.ppermute(tail, axis, [(i, (i + 1) % count) for i in range(ends)])  25.5 us
    mul x2, other arithmetic, dct_table(): (jnp.cos(outer_angle)[:, :, None] * jnp.cos(inner_angle)[:, None, :] - jn...  19.1 us
    dot_general x1, matrix products, spectral(): lax.dot_general(pixel_cube, table, (((0,), (1,)), ((), ())), precision=pr...  17.7 us
    sub x4, other arithmetic, synthesise(): operand = running - space_next[level_idx]  17.1 us
    unnamed x33, local copies, waits for them, and re-layouts  16.8 us
    mul x3, other arithmetic, analyse(): smoothed = smoothed * inside[:, start_row:start_row + out_rows, :]  16.2 us
    add x5, other arithmetic, blur_rows(): running = running + TAPS[tap_idx] * padded[:, offset:offset + out_rows, :]  15.9 us
  transfers between devices with their start and end apart: 12, of which 6 were waited for; matrix products, arithmetic and copies ran while one was open for 58% of the time, Pallas kernels for 0%

profile of v1, /device:TPU:0, one launch (start us, length us, event | category | flops | bytes accessed | tf_op | source)
XLA Modules:
  0.0 257.3 jit_solution(592620569219811965)
XLA Ops:
  0.6 3.0 %copy.22 = f32[128,32,128]{0,2,1:T(8,128)} copy(f32[128,32,128]{2,1,0:T(8,128)} %param.4) | data formatting | bytes 4194304 | tf_op args[0]
  3.6 7.6 %all-to-all-start = ((f32[128,16,256]{0,2,1:T(8,128)}), f32[128,16,256]{0,2,1:T(8,128)}, u32[]{:S(2)}, u32[]{:S(2)}) async-start(f32[128,16,256]{0,2,1:T(8,128)} %bitcast.58), calls=%async_computation | async-start | bytes 4194304 | tf_op jit(solution)/shard_map/all_to_all | solution.py:143
  11.8 2.4 copy.29
  14.2 1.3 collective-permute-start.1
  15.5 2.4 copy.28
  17.9 7.1 %collective-permute-start = (f32[128,30,128]{2,0,1:T(8,128)}, f32[128,30,128]{2,0,1:T(8,128)}, u32[]{:S(2)}, u32[]{:S(2)}) collective-permute-start(f32[128,30,128]{2,0,1:T(8,128)} %copy.28), channel_id=1, source_target_pairs={{0,1},{2,3},{4,5},{6,7},{8,9},{10,11},{12,13},{14,15},{16,17},{18,... | collective-permute-start | bytes 5898248 | tf_op jit(solution)/shard_map/ppermute | solution.py:26
  26.4 3.4 %copy.24 = f32[256,2048]{0,1:T(8,128)} copy(f32[256,2048]{1,0:T(8,128)} %param.7) | data formatting | bytes 4194304 | tf_op args[3]
  29.8 2.1 fusion.162
  31.9 12.0 %broadcast_multiply_fusion = (f32[2048,32,64]{0,2,1:T(8,128)}, f32[2048,32,64]{0,2,1:T(8,128)}) fusion(f32[2048]{0:T(1024)S(1)} %fusion.168, f32[2048,64]{0,1:T(8,128)S(1)} %get-tuple-element.44, f32[2048,32]{0,1:T(8,128)S(1)} %get-tuple-element.42, f32[2048,64]{0,1:T(8,128)S(1)} %get-tuple-element.43, f32[2048,32]{0,1:T(8,128)S(1)} %get-tuple-element.41), kind=kLoop, calls=%fused_computation.15 | loop fusion | flops 16777216 | bytes 35135488 | tf_op jit(solution)/shard_map/mul | solution.py:109
  43.9 17.6 %collective-permute-done.1 = f32[128,30,128]{2,0,1:T(8,128)} collective-permute-done((f32[128,30,128]{2,0,1:T(8,128)}, f32[128,30,128]{2,0,1:T(8,128)}, u32[]{:S(2)}, u32[]{:S(2)}) %collective-permute-start.1) | collective-permute-done | bytes 1966112 | tf_op jit(solution)/shard_map/ppermute | solution.py:28
  61.5 2.7 %copy.21 = f32[128,30,128]{2,1,0:T(8,128)S(1)} copy(f32[128,30,128]{2,0,1:T(8,128)} %collective-permute-done.1) | data formatting | bytes 3932160 | tf_op jit(solution)/shard_map/ppermute | solution.py:28
  64.2 2.2 collective-permute-done
  66.4 2.7 %copy.20 = f32[128,30,128]{2,1,0:T(8,128)S(1)} copy(f32[128,30,128]{2,0,1:T(8,128)} %collective-permute-done) | data formatting | bytes 3932160 | tf_op jit(solution)/shard_map/ppermute | solution.py:26
  69.8 4.8 %fusion.173 = (f32[128,88,128]{2,1,0:T(8,128)}, f32[128,88,128]{2,1,0:T(8,128)S(1)}) fusion(f32[128,92,128]{2,1,0:T(8,128)S(1)} %pad_maximum_fusion.1), kind=kLoop, calls=%fused_computation.266 | loop fusion | flops 12976128 | bytes 40370176 | tf_op jit(solution)/shard_map/slice | solution.py:39
  74.6 6.1 %fusion.5 = f32[128,88,128]{2,1,0:T(8,128)S(1)} fusion(f32[128,88,128]{2,1,0:T(8,128)S(1)} %get-tuple-element.24, f32[88]{0:T(128)S(1)} %slice_bitcast_fusion.3), kind=kLoop, calls=%fused_computation.42 | loop fusion | flops 14417920 | bytes 11534688 | tf_op jit(solution)/shard_map/mul | solution.py:75
  80.7 4.2 %fusion.174 = (f32[128,80,128]{2,1,0:T(8,128)}, f32[128,80,128]{2,1,0:T(8,128)S(1)}) fusion(f32[128,88,128]{2,1,0:T(8,128)S(1)} %fusion.5), kind=kLoop, calls=%fused_computation.267 | loop fusion | flops 11796480 | bytes 36700160 | tf_op jit(solution)/shard_map/slice | solution.py:39
  85.0 5.6 %fusion.18 = f32[128,80,128]{2,1,0:T(8,128)S(1)} fusion(f32[128,80,128]{2,1,0:T(8,128)S(1)} %get-tuple-element.26, f32[80]{0:T(128)S(1)} %slice_bitcast_fusion.2), kind=kLoop, calls=%fused_computation.59 | loop fusion | flops 13107200 | bytes 10486080 | tf_op jit(solution)/shard_map/mul | solution.py:75
  90.5 2.6 %fusion.175 = (f32[128,64,128]{2,1,0:T(8,128)S(1)}, f32[128,64,128]{2,1,0:T(8,128)S(1)}) fusion(f32[128,80,128]{2,1,0:T(8,128)S(1)} %fusion.18), kind=kLoop, calls=%fused_computation.268 | loop fusion | flops 9437184 | bytes 29360128 | tf_op jit(solution)/shard_map/slice | solution.py:39
  93.2 4.5 %fusion.31 = f32[128,64,128]{2,1,0:T(8,128)S(1)} fusion(f32[128,64,128]{2,1,0:T(8,128)S(1)} %get-tuple-element.28, f32[64]{0:T(128)S(1)} %slice_bitcast_fusion.1), kind=kLoop, calls=%fused_computation.76 | loop fusion | flops 10485760 | bytes 8388864 | tf_op jit(solution)/shard_map/mul | solution.py:75
  98.4 3.9 %broadcast_subtract_fusion = (f32[128,32,128]{2,1,0:T(8,128)S(1)}, f32[128,32,128]{2,1,0:T(8,128)S(1)}) fusion(f32[32]{0:T(128)S(1)} %slice_bitcast_fusion, f32[128,32,128]{2,1,0:T(8,128)S(1)} %fusion.148, f32[128,64,128]{2,1,0:T(8,128)S(1)} %fusion.31, f32[4,128,32,128]{3,2,1,0:T(8,128)} %param.6), kind=kLoop, calls=%fused_computation.234 | loop fusion | flops 7864320 | bytes 10485888 | tf_op jit(solution)/shard_map/sub | solution.py:88
  102.5 1.3 collective-permute-start.3
  103.8 4.7 %collective-permute-start.2 = (f32[128,16,128]{2,1,0:T(8,128)S(1)}, f32[128,16,128]{2,1,0:T(8,128)S(1)}, u32[]{:S(2)}, u32[]{:S(2)}) collective-permute-start(f32[128,16,128]{2,1,0:T(8,128)S(1)} %get-tuple-element.35), channel_id=1, source_target_pairs={{0,1},{2,3},{4,5},{6,7},{8,9},{10,11},{12,13},{14,15},{16,17},{18,... | collective-permute-start | bytes 3145736 | tf_op jit(solution)/shard_map/ppermute | solution.py:26
  108.5 7.2 %bitcast_multiply_fusion = f32[2048,2048]{0,1:T(8,128)} fusion(f32[2048,32,64]{0,2,1:T(8,128)S(1)} %bitcast.53, f32[2048]{0:T(1024)S(1)} %fusion.168), kind=kLoop, calls=%fused_computation.4 | loop fusion | flops 4194304 | bytes 33562624 | tf_op jit(solution)/shard_map/mul | solution.py:109
  115.7 13.1 %collective-permute-done.3 = f32[128,16,128]{2,1,0:T(8,128)S(1)} collective-permute-done((f32[128,16,128]{2,1,0:T(8,128)S(1)}, f32[128,16,128]{2,1,0:T(8,128)S(1)}, u32[]{:S(2)}, u32[]{:S(2)}) %collective-permute-start.3) | collective-permute-done | bytes 1048608 | tf_op jit(solution)/shard_map/ppermute | solution.py:28
  131.2 4.4 %fusion.93 = (f32[128,32,128]{2,1,0:T(8,128)S(1)}, f32[128,32,128]{2,1,0:T(8,128)}) fusion(f32[128,32,128]{2,1,0:T(8,128)S(1)} %get-tuple-element.22, f32[128,32,128]{2,1,0:T(8,128)S(1)} %fusion.69, f32[128,64,128]{2,1,0:T(8,128)S(1)} %fusion.31, f32[128,64,128]{2,1,0:T(8,128)S(1)} %get-tuple-element.27, f32[4,128,32,128]{3,2,1,0:T(8,128)} %param.6), kind=kLoop, calls=%fused_computation.160 | loop fusion | flops 7864320 | bytes 14680064 | tf_op jit(solution)/shard_map/sub | solution.py:88
  135.6 1.3 copy-done.8
  139.3 4.6 %collective-permute-start.4 = (f32[128,8,128]{2,1,0:T(8,128)}, f32[128,8,128]{2,1,0:T(8,128)S(1)}, u32[]{:S(2)}, u32[]{:S(2)}) collective-permute-start(f32[128,8,128]{2,1,0:T(8,128)} %get-tuple-element.33), channel_id=1, source_target_pairs={{0,1},{2,3},{4,5},{6,7},{8,9},{10,11},{12,13},{14,15},{16,17},{18,... | collective-permute-start | bytes 1572872 | tf_op jit(solution)/shard_map/ppermute | solution.py:26
  143.9 3.1 %copy.23 = f32[16,128,1,256]{3,1,0,2:T(8,128)} copy(f32[16,128,1,256]{1,3,0,2:T(8,128)} %bitcast.12) | data formatting | bytes 4194304 | tf_op jit(solution)/shard_map/all_to_all | solution.py:143
  147.0 17.7 %fusion.41 = f32[256,2048]{0,1:T(8,128)S(1)} fusion(f32[256,2048]{0,1:T(8,128)} %copy.24, f32[2048,2048]{0,1:T(8,128)} %bitcast.51, f32[2048,256]{1,0:T(8,128)} %bitcast.59), kind=kOutput, calls=%fused_computation.108 | convolution fusion | flops 6444023808 | bytes 23068672 | tf_op jit(solution)/shard_map/dot_general | solution.py:120
  164.8 10.9 %convolution_bitcast_fusion = f32[2048,1,256]{2,0,1:T(8,128)S(1)} fusion(f32[2048,2048]{0,1:T(8,128)} %bitcast_multiply_fusion, f32[256,2048]{0,1:T(8,128)S(1)} %fusion.41), kind=kOutput, calls=%fused_computation.94 | convolution fusion | flops 6442450944 | bytes 20971520 | tf_op jit(solution)/shard_map/dot_general | solution.py:128
  175.8 10.0 %copy.25 = f32[2048,1,256]{2,1,0:T(1,128)} copy(f32[2048,1,256]{2,0,1:T(8,128)S(1)} %convolution_bitcast_fusion) | data formatting | bytes 4194304 | tf_op jit(solution)/shard_map/reshape | solution.py:156
  185.7 5.8 %all-to-all-start.1 = ((f32[2048,1,256]{2,1,0:T(1,128)}), f32[2048,1,256]{2,1,0:T(1,128)}, u32[]{:S(2)}, u32[]{:S(2)}) async-start(f32[2048,1,256]{2,1,0:T(1,128)} %copy.25), calls=%async_computation.1 | async-start | bytes 4194304 | tf_op jit(solution)/shard_map/all_to_all | solution.py:155
  191.6 5.5 %fusion.61 = f32[128,32,128]{2,1,0:T(8,128)S(1)} fusion(f32[128,32,128]{2,1,0:T(8,128)} %copy-done.8, f32[128,8,128]{2,1,0:T(8,128)S(1)} %collective-permute-done.5, f32[128,8,128]{2,1,0:T(8,128)S(1)} %collective-permute-done.4), kind=kLoop, calls=%fused_computation.128 | loop fusion | flops 6815744 | bytes 5242880 | tf_op jit(solution)/shard_map/add | solution.py:39
  197.2 4.2 %fusion.103 = (f32[128,32,128]{2,1,0:T(8,128)S(1)}, f32[128,32,128]{2,1,0:T(8,128)S(1)}) fusion(f32[128,32,128]{2,1,0:T(8,128)S(1)} %copy-done.4, f32[128,32,128]{2,1,0:T(8,128)S(1)} %fusion.61, f32[128,80,128]{2,1,0:T(8,128)} %copy-done.1, f32[128,80,128]{2,1,0:T(8,128)} %get-tuple-element.25, f32[4,128,32,128]{3,2,1,0:T(8,128)} %param.6), kind=kLoop, calls=%fused_computation.170 | loop fusion | flops 7864320 | bytes 14680064 | tf_op jit(solution)/shard_map/sub | solution.py:88
  201.5 1.3 collective-permute-start.7
  202.8 4.6 %collective-permute-start.6 = (f32[128,4,128]{2,1,0:T(4,128)S(1)}, f32[128,4,128]{2,1,0:T(4,128)S(1)}, u32[]{:S(2)}, u32[]{:S(2)}) collective-permute-start(f32[128,4,128]{2,1,0:T(4,128)S(1)} %get-tuple-element.31), channel_id=1, source_target_pairs={{0,1},{2,3},{4,5},{6,7},{8,9},{10,11},{12,13},{14,15},{16,17},{18,... | collective-permute-start | bytes 786440 | tf_op jit(solution)/shard_map/ppermute | solution.py:26
  207.4 4.3 %collective-permute-done.7 = f32[128,4,128]{2,1,0:T(4,128)S(1)} collective-permute-done((f32[128,4,128]{2,1,0:T(4,128)S(1)}, f32[128,4,128]{2,1,0:T(4,128)S(1)}, u32[]{:S(2)}, u32[]{:S(2)}) %collective-permute-start.7) | collective-permute-done | bytes 262176 | tf_op jit(solution)/shard_map/ppermute | solution.py:28
  212.9 1.6 fusion.53
  214.5 4.6 %fusion.113 = (f32[128,32,128]{2,1,0:T(8,128)S(1)}, f32[128,32,128]{2,1,0:T(8,128)S(1)}) fusion(f32[128,32,128]{2,1,0:T(8,128)S(1)} %get-tuple-element.18, f32[128,32,128]{2,1,0:T(8,128)S(1)} %fusion.53, f32[128,88,128]{2,1,0:T(8,128)} %copy-done, f32[128,88,128]{2,1,0:T(8,128)} %get-tuple-element.23, f32[4,128,32,128]{3,2,1,0:T(8,128)} %param.6), kind=kLoop, calls=%fused_computation.180 | loop fusion | flops 7864320 | bytes 14680064 | tf_op jit(solution)/shard_map/sub | solution.py:88
  219.1 1.4 copy-done.9
  220.5 1.3 collective-permute-start.9
  221.8 4.6 %collective-permute-start.8 = (f32[128,2,128]{2,1,0:T(2,128)S(1)}, f32[128,2,128]{2,1,0:T(2,128)S(1)}, u32[]{:S(2)}, u32[]{:S(2)}) collective-permute-start(f32[128,2,128]{2,1,0:T(2,128)S(1)} %get-tuple-element.29), channel_id=1, source_target_pairs={{0,1},{2,3},{4,5},{6,7},{8,9},{10,11},{12,13},{14,15},{16,17},{18,... | collective-permute-start | bytes 393224 | tf_op jit(solution)/shard_map/ppermute | solution.py:26
  226.4 3.9 %pad_maximum_fusion = f32[4,128,32,128]{3,2,1,0:T(8,128)} fusion(f32[1,128,32,128]{3,2,1,0:T(8,128)S(1)} %bitcast.56, f32[1,128,32,128]{3,2,1,0:T(8,128)S(1)} %bitcast.54, f32[1,128,32,128]{3,2,1,0:T(8,128)S(1)} %bitcast.55, f32[1,128,32,128]{3,2,1,0:T(8,128)S(1)} %bitcast.57), kind=kLoop, calls=%fused_computation.14 | loop fusion | flops 6291456 | bytes 16777216 | tf_op jit(solution)/shard_map/stack | solution.py:147
  230.3 2.9 %copy.27 = f32[256,2048]{1,0:T(8,128)} copy(f32[256,2048]{0,1:T(8,128)} %copy-done.3) | data formatting | bytes 4194304
  233.1 7.1 %fusion.45 = f32[128,32,128]{2,1,0:T(8,128)} fusion(f32[128,32,128]{2,1,0:T(8,128)} %copy-done.9, f32[128,2,128]{2,1,0:T(2,128)S(1)} %collective-permute-done.9, f32[128,2,128]{2,1,0:T(2,128)S(1)} %collective-permute-done.8), kind=kLoop, calls=%fused_computation.112 | loop fusion | flops 6815744 | bytes 4456448 | tf_op jit(solution)/shard_map/add | solution.py:39
  240.2 4.1 %copy.26 = f32[128,16,1,256]{3,1,0,2:T(8,128)} copy(f32[128,16,1,256]{3,2,0,1:T(1,128)} %bitcast.17) | data formatting | bytes 4194304 | tf_op jit(solution)/shard_map/all_to_all | solution.py:155
  244.3 2.6 %reshape.195 = f32[128,32,128]{2,1,0:T(8,128)} reshape(f32[128,16,1,256]{3,1,0,2:T(8,128)} %copy.26) | data formatting | bytes 4194304 | tf_op jit(solution)/shard_map/reshape | solution.py:162
  247.0 9.8 %fusion.127 = f32[128,32,128]{2,1,0:T(8,128)} fusion(f32[128,32,128]{2,1,0:T(8,128)S(1)} %copy-done.2, f32[128,32,128]{2,1,0:T(8,128)} %reshape.195, f32[128,32,128]{2,1,0:T(8,128)} %param.5, f32[128,32,128]{2,1,0:T(8,128)} %copy-done.7, f32[128,32,128]{2,1,0:T(8,128)} %fusion.45), kind=kLoop, calls=%fused_computation.194 | loop fusion | flops 7864320 | bytes 12582912 | tf_op jit(solution)/shard_map/max | solution.py:163
  (53 shorter events, 9.7 us)
Async XLA Ops:
  3.6 7.6 %copy-start.2 = (f32[128,32,128]{2,1,0:T(8,128)S(1)}, f32[128,32,128]{2,1,0:T(8,128)}, u32[]{:S(2)}) copy-start(f32[128,32,128]{2,1,0:T(8,128)} %param.4) | copy-start | bytes 6291460
  3.6 140.3 %all-to-all-start = ((f32[128,16,256]{0,2,1:T(8,128)}), f32[128,16,256]{0,2,1:T(8,128)}, u32[]{:S(2)}, u32[]{:S(2)}) async-start(f32[128,16,256]{0,2,1:T(8,128)} %bitcast.58), calls=%async_computation | async-start | bytes 4194304 | tf_op jit(solution)/shard_map/all_to_all | solution.py:143
  14.2 47.3 %collective-permute-start.1 = (f32[128,30,128]{2,0,1:T(8,128)}, f32[128,30,128]{2,0,1:T(8,128)}, u32[]{:S(2)}, u32[]{:S(2)}) collective-permute-start(f32[128,30,128]{2,0,1:T(8,128)} %copy.29), channel_id=1, source_target_pairs={{1,0},{3,2},{5,4},{7,6},{9,8},{11,10},{13,12},{15,14},{17,16},{19,... | collective-permute-start | bytes 5898248 | tf_op jit(solution)/shard_map/ppermute | solution.py:28
  17.9 48.4 %collective-permute-start = (f32[128,30,128]{2,0,1:T(8,128)}, f32[128,30,128]{2,0,1:T(8,128)}, u32[]{:S(2)}, u32[]{:S(2)}) collective-permute-start(f32[128,30,128]{2,0,1:T(8,128)} %copy.28), channel_id=1, source_target_pairs={{0,1},{2,3},{4,5},{6,7},{8,9},{10,11},{12,13},{14,15},{16,17},{18,... | collective-permute-start | bytes 5898248 | tf_op jit(solution)/shard_map/ppermute | solution.py:26
  80.7 4.2 %copy-start = (f32[128,88,128]{2,1,0:T(8,128)}, f32[128,88,128]{2,1,0:T(8,128)S(1)}, u32[]{:S(2)}) copy-start(f32[128,88,128]{2,1,0:T(8,128)S(1)} %fusion.5) | copy-start | bytes 17301508
  90.5 2.7 %copy-start.1 = (f32[128,80,128]{2,1,0:T(8,128)}, f32[128,80,128]{2,1,0:T(8,128)S(1)}, u32[]{:S(2)}) copy-start(f32[128,80,128]{2,1,0:T(8,128)S(1)} %fusion.18) | copy-start | bytes 15728644
  93.2 15.3 %slice-start = ((s8[16777216]{0:T(1024)(128)(4,1)}), s8[4194304]{0:T(1024)(128)(4,1)S(1)}, s32[]{:S(2)}) async-start(s8[16777216]{0:T(1024)(128)(4,1)} %bitcast.52), calls=%async_computation.2 | async-start | bytes 8388608
  97.7 10.8 %slice-start.1 = ((s8[16777216]{0:T(1024)(128)(4,1)}), s8[4194304]{0:T(1024)(128)(4,1)S(1)}, s32[]{:S(2)}) async-start(s8[16777216]{0:T(1024)(128)(4,1)} %bitcast.52), calls=%async_computation.3 | async-start | bytes 8388608
  97.7 10.8 %slice-start.2 = ((s8[16777216]{0:T(1024)(128)(4,1)}), s8[4194304]{0:T(1024)(128)(4,1)S(1)}, s32[]{:S(2)}) async-start(s8[16777216]{0:T(1024)(128)(4,1)} %bitcast.52), calls=%async_computation.4 | async-start | bytes 8388608
  98.4 10.1 %slice-start.3 = ((s8[16777216]{0:T(1024)(128)(4,1)}), s8[4194304]{0:T(1024)(128)(4,1)S(1)}, s32[]{:S(2)}) async-start(s8[16777216]{0:T(1024)(128)(4,1)} %bitcast.52), calls=%async_computation.5 | async-start | bytes 8388608
  102.3 28.9 %copy-start.5 = (f32[128,32,128]{2,1,0:T(8,128)}, f32[128,32,128]{2,1,0:T(8,128)S(1)}, u32[]{:S(2)}) copy-start(f32[128,32,128]{2,1,0:T(8,128)S(1)} %get-tuple-element.22) | copy-start | bytes 6291460
  102.5 26.3 %collective-permute-start.3 = (f32[128,16,128]{2,1,0:T(8,128)S(1)}, f32[128,16,128]{2,1,0:T(8,128)S(1)}, u32[]{:S(2)}, u32[]{:S(2)}) collective-permute-start(f32[128,16,128]{2,1,0:T(8,128)S(1)} %get-tuple-element.36), channel_id=1, source_target_pairs={{1,0},{3,2},{5,4},{7,6},{9,8},{11,10},{13,12},{15,14},{17,16},{19,... | collective-permute-start | bytes 3145736 | tf_op jit(solution)/shard_map/ppermute | solution.py:28
  103.8 26.3 %collective-permute-start.2 = (f32[128,16,128]{2,1,0:T(8,128)S(1)}, f32[128,16,128]{2,1,0:T(8,128)S(1)}, u32[]{:S(2)}, u32[]{:S(2)}) collective-permute-start(f32[128,16,128]{2,1,0:T(8,128)S(1)} %get-tuple-element.35), channel_id=1, source_target_pairs={{0,1},{2,3},{4,5},{6,7},{8,9},{10,11},{12,13},{14,15},{16,17},{18,... | collective-permute-start | bytes 3145736 | tf_op jit(solution)/shard_map/ppermute | solution.py:26
  135.6 1.3 copy-start.8
  138.0 53.6 %collective-permute-start.5 = (f32[128,8,128]{2,1,0:T(8,128)}, f32[128,8,128]{2,1,0:T(8,128)S(1)}, u32[]{:S(2)}, u32[]{:S(2)}) collective-permute-start(f32[128,8,128]{2,1,0:T(8,128)} %get-tuple-element.34), channel_id=1, source_target_pairs={{1,0},{3,2},{5,4},{7,6},{9,8},{11,10},{13,12},{15,14},{17,16},{19,... | collective-permute-start | bytes 1572872 | tf_op jit(solution)/shard_map/ppermute | solution.py:28
  139.3 52.3 %collective-permute-start.4 = (f32[128,8,128]{2,1,0:T(8,128)}, f32[128,8,128]{2,1,0:T(8,128)S(1)}, u32[]{:S(2)}, u32[]{:S(2)}) collective-permute-start(f32[128,8,128]{2,1,0:T(8,128)} %get-tuple-element.33), channel_id=1, source_target_pairs={{0,1},{2,3},{4,5},{6,7},{8,9},{10,11},{12,13},{14,15},{16,17},{18,... | collective-permute-start | bytes 1572872 | tf_op jit(solution)/shard_map/ppermute | solution.py:26
  164.8 11.0 %copy-start.3 = (f32[256,2048]{0,1:T(8,128)}, f32[256,2048]{0,1:T(8,128)S(1)}, u32[]{:S(2)}) copy-start(f32[256,2048]{0,1:T(8,128)S(1)} %fusion.41) | copy-start | bytes 6291460
  185.7 54.5 %all-to-all-start.1 = ((f32[2048,1,256]{2,1,0:T(1,128)}), f32[2048,1,256]{2,1,0:T(1,128)}, u32[]{:S(2)}, u32[]{:S(2)}) async-start(f32[2048,1,256]{2,1,0:T(1,128)} %copy.25), calls=%async_computation.1 | async-start | bytes 4194304 | tf_op jit(solution)/shard_map/all_to_all | solution.py:155
  191.6 5.6 %copy-start.4 = (f32[128,32,128]{2,1,0:T(8,128)S(1)}, f32[128,32,128]{2,1,0:T(8,128)}, u32[]{:S(2)}) copy-start(f32[128,32,128]{2,1,0:T(8,128)} %get-tuple-element.20) | copy-start | bytes 6291460
  201.5 10.2 %collective-permute-start.7 = (f32[128,4,128]{2,1,0:T(4,128)S(1)}, f32[128,4,128]{2,1,0:T(4,128)S(1)}, u32[]{:S(2)}, u32[]{:S(2)}) collective-permute-start(f32[128,4,128]{2,1,0:T(4,128)S(1)} %get-tuple-element.32), channel_id=1, source_target_pairs={{1,0},{3,2},{5,4},{7,6},{9,8},{11,10},{13,12},{15,14},{17,16},{19,... | collective-permute-start | bytes 786440 | tf_op jit(solution)/shard_map/ppermute | solution.py:28
  202.8 10.1 %collective-permute-start.6 = (f32[128,4,128]{2,1,0:T(4,128)S(1)}, f32[128,4,128]{2,1,0:T(4,128)S(1)}, u32[]{:S(2)}, u32[]{:S(2)}) collective-permute-start(f32[128,4,128]{2,1,0:T(4,128)S(1)} %get-tuple-element.31), channel_id=1, source_target_pairs={{0,1},{2,3},{4,5},{6,7},{8,9},{10,11},{12,13},{14,15},{16,17},{18,... | collective-permute-start | bytes 786440 | tf_op jit(solution)/shard_map/ppermute | solution.py:26
  214.4 11.9 %copy-start.6 = (f32[128,32,128]{2,1,0:T(8,128)S(1)}, f32[128,32,128]{2,1,0:T(8,128)}, u32[]{:S(2)}) copy-start(f32[128,32,128]{2,1,0:T(8,128)} %copy-done.5) | copy-start | bytes 6291460
  219.0 1.4 copy-start.9
  219.0 7.3 %copy-start.7 = (f32[128,32,128]{2,1,0:T(8,128)}, f32[128,32,128]{2,1,0:T(8,128)S(1)}, u32[]{:S(2)}) copy-start(f32[128,32,128]{2,1,0:T(8,128)S(1)} %get-tuple-element.16) | copy-start | bytes 6291460
  220.5 12.6 %collective-permute-start.9 = (f32[128,2,128]{2,1,0:T(2,128)S(1)}, f32[128,2,128]{2,1,0:T(2,128)S(1)}, u32[]{:S(2)}, u32[]{:S(2)}) collective-permute-start(f32[128,2,128]{2,1,0:T(2,128)S(1)} %get-tuple-element.30), channel_id=1, source_target_pairs={{1,0},{3,2},{5,4},{7,6},{9,8},{11,10},{13,12},{15,14},{17,16},{19,... | collective-permute-start | bytes 393224 | tf_op jit(solution)/shard_map/ppermute | solution.py:28
  221.8 11.3 %collective-permute-start.8 = (f32[128,2,128]{2,1,0:T(2,128)S(1)}, f32[128,2,128]{2,1,0:T(2,128)S(1)}, u32[]{:S(2)}, u32[]{:S(2)}) collective-permute-start(f32[128,2,128]{2,1,0:T(2,128)S(1)} %get-tuple-element.29), channel_id=1, source_target_pairs={{0,1},{2,3},{4,5},{6,7},{8,9},{10,11},{12,13},{14,15},{16,17},{18,... | collective-permute-start | bytes 393224 | tf_op jit(solution)/shard_map/ppermute | solution.py:26

commit v2 on v1

--- a/solution.py
+++ b/solution.py
@@ -4,6 +4,8 @@
 import jax.numpy as jnp
 from jax import lax
 from jax.sharding import PartitionSpec as P
+from jax.experimental import pallas as pl
+from jax.experimental.pallas import tpu as pltpu
 
 SCALES = 4
 
@@ -135,6 +137,85 @@
     return (running, freq_next)
 
 
+def smooth_block(x, dilation, inside, lane):
+    rows, columns = x.shape
+    near = pltpu.roll(x, dilation, 0) + pltpu.roll(x, rows - dilation, 0)
+    far = pltpu.roll(x, 2 * dilation, 0) + pltpu.roll(x, rows - 2 * dilation, 0)
+    y = TAPS[0] * far + TAPS[1] * near + TAPS[2] * x
+    zero = jnp.zeros_like(y)
+    near = jnp.where(lane >= dilation, pltpu.roll(y, dilation, 1), zero) + jnp.where(
+        lane < columns - dilation, pltpu.roll(y, columns - dilation, 1), zero
+    )
+    far = jnp.where(lane >= 2 * dilation, pltpu.roll(y, 2 * dilation, 1), zero) + jnp.where(
+        lane < columns - 2 * dilation, pltpu.roll(y, columns - 2 * dilation, 1), zero
+    )
+    z = TAPS[0] * far + TAPS[1] * near + TAPS[2] * y
+    return z * inside
+
+
+def starlet_kernel(top_ref, mid_ref, bot_ref, duals_ref, inside_ref, sn_ref, ttop_ref, tmid_ref, tbot_ref):
+    block, local_rows, columns = mid_ref.shape
+    extent = 3 * local_rows
+    inside = inside_ref[...]
+    lane = lax.broadcasted_iota(jnp.int32, (extent, columns), 1)
+    pad = jnp.zeros((local_rows, columns), jnp.float32)
+
+    def body(ch, carry):
+        current = jnp.concatenate([top_ref[ch], mid_ref[ch], bot_ref[ch]], axis=0)
+        fresh = []
+        for level_idx in range(SCALES):
+            smoothed = smooth_block(current, 2**level_idx, inside, lane)
+            detail = (current - smoothed)[local_rows : 2 * local_rows]
+            plane = jnp.clip(duals_ref[level_idx, ch] + SIGMA * detail, -SPACE_BOUND, SPACE_BOUND)
+            sn_ref[level_idx, ch] = plane
+            fresh.append(plane)
+            current = smoothed
+        running = jnp.zeros((extent, columns), jnp.float32)
+        for level_idx in reversed(range(SCALES)):
+            plane = jnp.concatenate([pad, fresh[level_idx], pad], axis=0)
+            running = smooth_block(running - plane, 2**level_idx, inside, lane) + plane
+        ttop_ref[ch] = running[0:local_rows]
+        tmid_ref[ch] = running[local_rows : 2 * local_rows]
+        tbot_ref[ch] = running[2 * local_rows : extent]
+        return carry
+
+    lax.fori_loop(0, block, body, 0)
+
+
+def starlet(above, image_cube, below, space_duals, inside, interpret=False):
+    chans, local_rows, columns = image_cube.shape
+    block = math.gcd(chans, 8)
+    extent = 3 * local_rows
+    plane_spec = pl.BlockSpec((block, local_rows, columns), lambda i: (i, 0, 0))
+    dual_spec = pl.BlockSpec((SCALES, block, local_rows, columns), lambda i: (0, i, 0, 0))
+    plane_shape = jax.ShapeDtypeStruct(image_cube.shape, jnp.float32)
+    return pl.pallas_call(
+        starlet_kernel,
+        grid=(chans // block,),
+        in_specs=[plane_spec, plane_spec, plane_spec, dual_spec, pl.BlockSpec((extent, columns), lambda i: (0, 0))],
+        out_specs=[dual_spec, plane_spec, plane_spec, plane_spec],
+        out_shape=[jax.ShapeDtypeStruct(space_duals.shape, jnp.float32), plane_shape, plane_shape, plane_shape],
+        interpret=interpret,
+    )(above, image_cube, below, space_duals, inside)
+
+
+def spatial(image_cube, space_duals):
+    chans, local_rows, columns = image_cube.shape
+    assert local_rows >= 2 ** (SCALES + 1) - 2
+    count = lax.axis_size("rows")
+    down = [(i, i + 1) for i in range(count - 1)]
+    up = [(i + 1, i) for i in range(count - 1)]
+    above = lax.ppermute(image_cube, "rows", down)
+    below = lax.ppermute(image_cube, "rows", up)
+    first_row = (lax.axis_index("rows") - 1) * local_rows
+    positions = first_row + jnp.arange(3 * local_rows, dtype=jnp.int32)
+    inside = ((positions >= 0) & (positions < local_rows * count)).astype(jnp.float32)
+    inside = jnp.broadcast_to(inside[:, None], (3 * local_rows, columns))
+    space_next, spill_up, own, spill_down = starlet(above, image_cube, below, space_duals, inside)
+    space_term = own + lax.ppermute(spill_down, "rows", down) + lax.ppermute(spill_up, "rows", up)
+    return space_term, space_next
+
+
 def local(image_cube, data_grad, space_duals, freq_duals):
     chans, local_rows, columns = image_cube.shape
     peers = lax.axis_size("freq")
@@ -143,14 +224,7 @@
     pixel_cube = lax.all_to_all(pieces, "freq", split_axis=1, concat_axis=0, tiled=True).reshape(
         chans * peers, share
     )
-    details = analyse(image_cube)
-    space_next = jnp.stack(
-        [
-            jnp.clip(space_duals[level_idx] + SIGMA * details[level_idx], -SPACE_BOUND, SPACE_BOUND)
-            for level_idx in range(SCALES)
-        ]
-    )
-    space_term = synthesise(space_next)
+    space_term, space_next = spatial(image_cube, space_duals)
     spectral_sum, freq_next = spectral(pixel_cube, freq_duals)
     returned = lax.all_to_all(
         spectral_sum.reshape(chans * peers, 1, share),

time: 262 us -> 289 us (1.10)
  the two profiles are of different devices: /device:TPU:0 before, /device:TPU:13 now
where the time goes in v2:
time: 289 us; the launch traced here: 287 us
  Pallas kernels  117 us (40%)
  waiting for transfers between devices  64.9 us (22%)
  local copies, waits for them, and re-layouts  27.3 us (9%)
  starting transfers between devices  25.7 us (9%)
  matrix products  25.6 us (9%)
  other arithmetic  25 us (9%)
    pallas_call x1, Pallas kernels, starlet(): pl.pallas_call(starlet_kernel, grid=(chans // block,), in_specs=[plane_sp...  117 us
    ppermute x1, waiting for transfers between devices, spatial(): lax.ppermute(spill_down, 'rows', down)  33.3 us
    all_to_all x1, waiting for transfers between devices, local(): lax.all_to_all(pieces, 'freq', split_axis=1, concat_axis=0, tiled=True)  26.4 us
    dot_general x1, matrix products, spectral(): lax.dot_general(pixel_cube, table, (((0,), (1,)), ((), ())), precision=pr...  18.1 us
    mul x2, other arithmetic, dct_table(): (jnp.cos(outer_angle)[:, :, None] * jnp.cos(inner_angle)[:, None, :] - jn...  14.9 us
    reshape x1, local copies, waits for them, and re-layouts, local(): spectral_sum.reshape(chans * peers, 1, share)  9.98 us
    unnamed x7, local copies, waits for them, and re-layouts  7.94 us
    dot_general x1, matrix products, spectral(): lax.dot_general(table, freq_next, (((0,), (1,)), ((), ())), precision=pre...  7.52 us
  transfers between devices with their start and end apart: 6, of which 3 were waited for; matrix products, arithmetic and copies ran while one was open for 25% of the time, Pallas kernels for 41%

profile of v2, /device:TPU:13, one launch (start us, length us, event | category | flops | bytes accessed | tf_op | source)
XLA Modules:
  0.0 286.8 jit_solution(14895725767322939131)
XLA Ops:
  0.6 4.5 %collective-permute-start = (f32[128,32,128]{2,1,0:T(8,128)}, f32[128,32,128]{2,1,0:T(8,128)}, u32[]{:S(2)}, u32[]{:S(2)}) collective-permute-start(f32[128,32,128]{2,1,0:T(8,128)} %mid_ref.1), channel_id=1, source_target_pairs={{0,1},{2,3},{4,5},{6,7},{8,9},{10,11},{12,13},{14,15},{16,17},{18,... | collective-permute-start | bytes 6291464 | tf_op jit(solution)/shard_map/ppermute | solution.py:208
  5.1 1.3 collective-permute-start.1
  6.4 3.0 %copy.18 = f32[128,32,128]{0,2,1:T(8,128)} copy(f32[128,32,128]{2,1,0:T(8,128)} %mid_ref.1) | data formatting | bytes 4194304 | tf_op args[0]
  9.3 6.8 %all-to-all-start = ((f32[128,16,256]{0,2,1:T(8,128)}), f32[128,16,256]{0,2,1:T(8,128)S(1)}, u32[]{:S(2)}, u32[]{:S(2)}) async-start(f32[128,16,256]{0,2,1:T(8,128)} %bitcast.30), calls=%async_computation | async-start | bytes 4194304 | tf_op jit(solution)/shard_map/all_to_all | solution.py:224
  16.2 2.9 %copy.20 = f32[256,2048]{0,1:T(8,128)} copy(f32[256,2048]{1,0:T(8,128)} %param.7) | data formatting | bytes 4194304 | tf_op args[3]
  19.1 1.1 fusion.18
  20.2 2.1 fusion.13
  22.3 7.7 %broadcast_multiply_fusion = (f32[2048,32,64]{0,2,1:T(8,128)}, f32[2048,32,64]{0,2,1:T(8,128)S(1)}) fusion(f32[2048]{0:T(1024)S(1)} %fusion.19, f32[2048,64]{0,1:T(8,128)S(1)} %get-tuple-element.28, f32[2048,32]{0,1:T(8,128)S(1)} %get-tuple-element.26, f32[2048,64]{0,1:T(8,128)S(1)} %get-tuple-element.27, f32[2048,32]{0,1:T(8,128)S(1)} %get-tuple-element.25), kind=kLoop, calls=%fused_computation.2 | loop fusion | flops 16777216 | bytes 35135488 | tf_op jit(solution)/shard_map/mul | solution.py:111
  30.0 7.2 %bitcast_multiply_fusion = f32[2048,2048]{0,1:T(8,128)} fusion(f32[2048,32,64]{0,2,1:T(8,128)S(1)} %get-tuple-element.24, f32[2048]{0:T(1024)S(1)} %fusion.19), kind=kLoop, calls=%fused_computation | loop fusion | flops 4194304 | bytes 33562624 | tf_op jit(solution)/shard_map/mul | solution.py:111
  37.2 26.4 %all-to-all-done = f32[128,16,256]{0,2,1:T(8,128)S(1)} async-done(((f32[128,16,256]{0,2,1:T(8,128)}), f32[128,16,256]{0,2,1:T(8,128)S(1)}, u32[]{:S(2)}, u32[]{:S(2)}) %all-to-all-start) | async-done | bytes 2097184 | tf_op jit(solution)/shard_map/all_to_all | solution.py:224
  63.6 1.8 copy.19
  65.4 0.0 copy-start
  65.4 18.1 %fusion.2 = f32[256,2048]{0,1:T(8,128)S(1)} fusion(f32[256,2048]{0,1:T(8,128)} %copy.20, f32[2048,2048]{0,1:T(8,128)} %bitcast.28, f32[2048,256]{1,0:T(8,128)} %bitcast.32), kind=kOutput, calls=%fused_computation.7 | convolution fusion | flops 6444023808 | bytes 23068672 | tf_op jit(solution)/shard_map/dot_general | solution.py:122
  83.5 0.0 copy-done
  83.5 7.5 %convolution_bitcast_fusion = f32[2048,1,256]{2,0,1:T(8,128)S(1)} fusion(f32[2048,2048]{0,1:T(8,128)S(1)} %copy-done, f32[256,2048]{0,1:T(8,128)S(1)} %fusion.2), kind=kOutput, calls=%fused_computation.5 | convolution fusion | flops 6442450944 | bytes 20971520 | tf_op jit(solution)/shard_map/dot_general | solution.py:130
  91.0 10.0 %copy.21 = f32[2048,1,256]{2,1,0:T(1,128)} copy(f32[2048,1,256]{2,0,1:T(8,128)S(1)} %convolution_bitcast_fusion) | data formatting | bytes 4194304 | tf_op jit(solution)/shard_map/reshape | solution.py:230
  101.0 4.9 %all-to-all-start.1 = ((f32[2048,1,256]{2,1,0:T(1,128)}), f32[2048,1,256]{2,1,0:T(1,128)}, u32[]{:S(2)}, u32[]{:S(2)}) async-start(f32[2048,1,256]{2,1,0:T(1,128)} %copy.21), calls=%async_computation.1 | async-start | bytes 4194304 | tf_op jit(solution)/shard_map/all_to_all | solution.py:229
  105.9 0.0 collective-permute-done.top_ref
  105.9 0.0 collective-permute-done.1.bot_ref
  105.9 0.7 broadcast_in_dim.8.inside_ref
  106.6 117.5 %shard_map.67 = (f32[4,128,32,128]{3,2,1,0:T(8,128)}, f32[128,32,128]{2,1,0:T(8,128)}, f32[128,32,128]{2,1,0:T(8,128)}, f32[128,32,128]{2,1,0:T(8,128)}) custom-call(f32[128,32,128]{2,1,0:T(8,128)} %collective-permute-done.top_ref, f32[128,32,128]{2,1,0:T(8,128)} %mid_ref.1, f32[128,32,128]{2,1,0:T(8,128)} %collective-permute-done.1.bot_ref, ...), custom_call_target="tpu_custom_call" | custom-call | tf_op jit(solution)/shard_map/pallas_call | solution.py:192
  224.1 7.0 %collective-permute-start.2 = (f32[128,32,128]{2,1,0:T(8,128)}, f32[128,32,128]{2,1,0:T(8,128)}, u32[]{:S(2)}, u32[]{:S(2)}) collective-permute-start(f32[128,32,128]{2,1,0:T(8,128)} %get-tuple-element.8), channel_id=1, source_target_pairs={{0,1},{2,3},{4,5},{6,7},{8,9},{10,11},{12,13},{14,15},{16,17},{18,... | collective-permute-start | bytes 6291464 | tf_op jit(solution)/shard_map/ppermute | solution.py:215
  231.1 1.3 collective-permute-start.3
  232.4 2.1 copy.23
  234.4 0.0 all-to-all-done.1
  234.4 4.1 %copy.25 = f32[16,128,1,256]{3,0,1,2:T(8,128)} copy(f32[16,128,1,256]{3,2,1,0:T(1,128)} %bitcast.8) | data formatting | bytes 4194304 | tf_op jit(solution)/shard_map/all_to_all | solution.py:229
  238.6 0.0 copy-start.1
  238.6 2.8 reshape.184
  241.4 33.3 %collective-permute-done.2 = f32[128,32,128]{2,1,0:T(8,128)} collective-permute-done((f32[128,32,128]{2,1,0:T(8,128)}, f32[128,32,128]{2,1,0:T(8,128)}, u32[]{:S(2)}, u32[]{:S(2)}) %collective-permute-start.2) | collective-permute-done | bytes 2097184 | tf_op jit(solution)/shard_map/ppermute | solution.py:215
  274.7 5.1 %collective-permute-done.3 = f32[128,32,128]{2,1,0:T(8,128)} collective-permute-done((f32[128,32,128]{2,1,0:T(8,128)}, f32[128,32,128]{2,1,0:T(8,128)}, u32[]{:S(2)}, u32[]{:S(2)}) %collective-permute-start.3) | collective-permute-done | bytes 2097184 | tf_op jit(solution)/shard_map/ppermute | solution.py:215
  279.8 0.0 copy-done.1
  279.8 7.0 %subtract_maximum_fusion = f32[128,32,128]{2,1,0:T(8,128)} fusion(f32[128,32,128]{2,1,0:T(8,128)S(1)} %copy-done.1, f32[128,32,128]{2,1,0:T(8,128)} %reshape.184, f32[128,32,128]{2,1,0:T(8,128)} %param.5, f32[128,32,128]{2,1,0:T(8,128)} %collective-permute-done.3, f32[128,32,128]{2,1,0:T(8,128)} %get-tuple-element.7, f32[128,32,128]{2,1,0:T(8,128)} %collective-permute-done.2), kind=kLoop, calls=%fused_computation.9 | loop fusion | flops 3670016 | bytes 14680064 | tf_op jit(solution)/shard_map/max | solution.py:237
  (4 shorter events, 0.0 us)
Async XLA Ops:
  0.6 105.3 %collective-permute-start = (f32[128,32,128]{2,1,0:T(8,128)}, f32[128,32,128]{2,1,0:T(8,128)}, u32[]{:S(2)}, u32[]{:S(2)}) collective-permute-start(f32[128,32,128]{2,1,0:T(8,128)} %mid_ref.1), channel_id=1, source_target_pairs={{0,1},{2,3},{4,5},{6,7},{8,9},{10,11},{12,13},{14,15},{16,17},{18,... | collective-permute-start | bytes 6291464 | tf_op jit(solution)/shard_map/ppermute | solution.py:208
  5.1 100.8 %collective-permute-start.1 = (f32[128,32,128]{2,1,0:T(8,128)}, f32[128,32,128]{2,1,0:T(8,128)}, u32[]{:S(2)}, u32[]{:S(2)}) collective-permute-start(f32[128,32,128]{2,1,0:T(8,128)} %mid_ref.1), channel_id=1, source_target_pairs={{1,0},{3,2},{5,4},{7,6},{9,8},{11,10},{13,12},{15,14},{17,16},{19,... | collective-permute-start | bytes 6291464 | tf_op jit(solution)/shard_map/ppermute | solution.py:209
  9.3 54.3 %all-to-all-start = ((f32[128,16,256]{0,2,1:T(8,128)}), f32[128,16,256]{0,2,1:T(8,128)S(1)}, u32[]{:S(2)}, u32[]{:S(2)}) async-start(f32[128,16,256]{0,2,1:T(8,128)} %bitcast.30), calls=%async_computation | async-start | bytes 4194304 | tf_op jit(solution)/shard_map/all_to_all | solution.py:224
  65.4 18.1 %copy-start = (f32[2048,2048]{0,1:T(8,128)S(1)}, f32[2048,2048]{0,1:T(8,128)}, u32[]{:S(2)}) copy-start(f32[2048,2048]{0,1:T(8,128)} %bitcast_multiply_fusion) | copy-start | bytes 50331652
  101.0 133.4 %all-to-all-start.1 = ((f32[2048,1,256]{2,1,0:T(1,128)}), f32[2048,1,256]{2,1,0:T(1,128)}, u32[]{:S(2)}, u32[]{:S(2)}) async-start(f32[2048,1,256]{2,1,0:T(1,128)} %copy.21), calls=%async_computation.1 | async-start | bytes 4194304 | tf_op jit(solution)/shard_map/all_to_all | solution.py:229
  224.1 50.6 %collective-permute-start.2 = (f32[128,32,128]{2,1,0:T(8,128)}, f32[128,32,128]{2,1,0:T(8,128)}, u32[]{:S(2)}, u32[]{:S(2)}) collective-permute-start(f32[128,32,128]{2,1,0:T(8,128)} %get-tuple-element.8), channel_id=1, source_target_pairs={{0,1},{2,3},{4,5},{6,7},{8,9},{10,11},{12,13},{14,15},{16,17},{18,... | collective-permute-start | bytes 6291464 | tf_op jit(solution)/shard_map/ppermute | solution.py:215
  231.1 48.7 %collective-permute-start.3 = (f32[128,32,128]{2,1,0:T(8,128)}, f32[128,32,128]{2,1,0:T(8,128)}, u32[]{:S(2)}, u32[]{:S(2)}) collective-permute-start(f32[128,32,128]{2,1,0:T(8,128)} %get-tuple-element.9), channel_id=1, source_target_pairs={{1,0},{3,2},{5,4},{7,6},{9,8},{11,10},{13,12},{15,14},{17,16},{19,... | collective-permute-start | bytes 6291464 | tf_op jit(solution)/shard_map/ppermute | solution.py:215
  238.6 41.2 %copy-start.1 = (f32[128,32,128]{2,1,0:T(8,128)S(1)}, f32[128,32,128]{2,1,0:T(8,128)}, u32[]{:S(2)}) copy-start(f32[128,32,128]{2,1,0:T(8,128)} %mid_ref.1) | copy-start | bytes 6291460

commit v3 on v1

--- a/solution.py
+++ b/solution.py
@@ -4,6 +4,8 @@
 import jax.numpy as jnp
 from jax import lax
 from jax.sharding import PartitionSpec as P
+from jax.experimental import pallas as pl
+from jax.experimental.pallas import tpu as pltpu
 
 SCALES = 4
 
@@ -135,6 +137,130 @@
     return (running, freq_next)
 
 
+def starlet_kernel(first_ref, above_ref, own_ref, below_ref, duals_ref, sn_ref, top_ref, mid_ref, bot_ref, buf_a, buf_b):
+    halo, block, columns = above_ref.shape
+    local_rows = own_ref.shape[0]
+    extent = 2 * halo + local_rows
+    pad = 2 ** SCALES
+    total_rows = first_ref[1]
+    row0 = first_ref[0] - halo
+    lane = lax.broadcasted_iota(jnp.int32, (block, columns), 1)
+    weights = {}
+    for level_idx in range(SCALES):
+        dilation = 2**level_idx
+        weights[dilation] = tuple(
+            jnp.where(keep, tap, 0.0).astype(jnp.float32)
+            for step, tap in ((dilation, TAPS[1]), (2 * dilation, TAPS[0]))
+            for keep in (lane >= step, lane < columns - step)
+        )
+
+    def smooth_rows(src, dst, dilation, lo, hi):
+        near_w, far_w = weights[dilation][0:2], weights[dilation][2:4]
+
+        def body(e, carry):
+            at = e + pad
+            y = TAPS[0] * (src[at - 2 * dilation] + src[at + 2 * dilation]) + TAPS[1] * (
+                src[at - dilation] + src[at + dilation]
+            ) + TAPS[2] * src[at]
+            z = (
+                pltpu.roll(y, dilation, 1) * near_w[0]
+                + pltpu.roll(y, columns - dilation, 1) * near_w[1]
+                + pltpu.roll(y, 2 * dilation, 1) * far_w[0]
+                + pltpu.roll(y, columns - 2 * dilation, 1) * far_w[1]
+                + TAPS[2] * y
+            )
+            row = row0 + e
+            dst[at] = jnp.where((row >= 0) & (row < total_rows), z, 0.0)
+            return carry
+
+        lax.fori_loop(lo, hi, body, 0)
+
+    buf_a[...] = jnp.zeros_like(buf_a)
+    buf_a[pl.ds(pad, halo)] = above_ref[...]
+    buf_a[pl.ds(pad + halo, local_rows)] = own_ref[...]
+    buf_a[pl.ds(pad + halo + local_rows, halo)] = below_ref[...]
+    bufs = (buf_a, buf_b)
+    lo, hi = 0, extent
+    for level_idx in range(SCALES):
+        dilation = 2**level_idx
+        src, dst = bufs[level_idx % 2], bufs[(level_idx + 1) % 2]
+        lo, hi = lo + 2 * dilation, hi - 2 * dilation
+        smooth_rows(src, dst, dilation, lo, hi)
+
+        def detail_body(r, carry, src=src, dst=dst, level_idx=level_idx):
+            at = pad + halo + r
+            sn_ref[level_idx, r] = jnp.clip(
+                duals_ref[level_idx, r] + SIGMA * (src[at] - dst[at]), -SPACE_BOUND, SPACE_BOUND
+            )
+            return carry
+
+        lax.fori_loop(0, local_rows, detail_body, 0)
+
+    buf_a[...] = jnp.zeros_like(buf_a)
+    buf_b[...] = jnp.zeros_like(buf_b)
+    lo, hi = halo, halo + local_rows
+    for count, level_idx in enumerate(reversed(range(SCALES))):
+        dilation = 2**level_idx
+        src, dst = bufs[count % 2], bufs[(count + 1) % 2]
+        own = pl.ds(pad + halo, local_rows)
+        src[own] = src[own] - sn_ref[level_idx]
+        lo, hi = lo - 2 * dilation, hi + 2 * dilation
+        smooth_rows(src, dst, dilation, max(lo, 0), min(hi, extent))
+        dst[own] = dst[own] + sn_ref[level_idx]
+    top_ref[...] = dst[pl.ds(pad, halo)]
+    mid_ref[...] = dst[pl.ds(pad + halo, local_rows)]
+    bot_ref[...] = dst[pl.ds(pad + halo + local_rows, halo)]
+
+
+def starlet(first, above, own, below, duals, interpret=False):
+    halo, chans, columns = above.shape
+    local_rows = own.shape[0]
+    block = math.gcd(chans, 8)
+    extent = 2 * halo + local_rows + 2 * 2**SCALES
+    edge_spec = pl.BlockSpec((halo, block, columns), lambda i: (0, i, 0))
+    own_spec = pl.BlockSpec((local_rows, block, columns), lambda i: (0, i, 0))
+    dual_spec = pl.BlockSpec((SCALES, local_rows, block, columns), lambda i: (0, 0, i, 0))
+    edge_shape = jax.ShapeDtypeStruct(above.shape, jnp.float32)
+    return pl.pallas_call(
+        starlet_kernel,
+        grid=(chans // block,),
+        in_specs=[pl.BlockSpec(memory_space=pltpu.SMEM), edge_spec, own_spec, edge_spec, dual_spec],
+        out_specs=[dual_spec, edge_spec, own_spec, edge_spec],
+        out_shape=[
+            jax.ShapeDtypeStruct(duals.shape, jnp.float32),
+            edge_shape,
+            jax.ShapeDtypeStruct(own.shape, jnp.float32),
+            edge_shape,
+        ],
+        scratch_shapes=[pltpu.VMEM((extent, block, columns), jnp.float32)] * 2,
+        interpret=interpret,
+    )(first, above, own, below, duals)
+
+
+def spatial(image_cube, space_duals):
+    chans, local_rows, columns = image_cube.shape
+    halo = 2 ** (SCALES + 1) - 2
+    assert local_rows >= halo
+    count = lax.axis_size("rows")
+    down = [(i, i + 1) for i in range(count - 1)]
+    up = [(i + 1, i) for i in range(count - 1)]
+    own = jnp.transpose(image_cube, (1, 0, 2))
+    duals = jnp.transpose(space_duals, (0, 2, 1, 3))
+    above = lax.ppermute(own[local_rows - halo :], "rows", down)
+    below = lax.ppermute(own[:halo], "rows", up)
+    first = jnp.stack([lax.axis_index("rows") * local_rows, count * local_rows]).astype(jnp.int32)
+    space_next, spill_up, mid, spill_down = starlet(first, above, own, below, duals)
+    from_above = lax.ppermute(spill_down, "rows", down)
+    from_below = lax.ppermute(spill_up, "rows", up)
+    gap = local_rows - halo
+    space_term = (
+        mid
+        + jnp.pad(from_above, ((0, gap), (0, 0), (0, 0)))
+        + jnp.pad(from_below, ((gap, 0), (0, 0), (0, 0)))
+    )
+    return jnp.transpose(space_term, (1, 0, 2)), jnp.transpose(space_next, (0, 2, 1, 3))
+
+
 def local(image_cube, data_grad, space_duals, freq_duals):
     chans, local_rows, columns = image_cube.shape
     peers = lax.axis_size("freq")
@@ -143,14 +269,7 @@
     pixel_cube = lax.all_to_all(pieces, "freq", split_axis=1, concat_axis=0, tiled=True).reshape(
         chans * peers, share
     )
-    details = analyse(image_cube)
-    space_next = jnp.stack(
-        [
-            jnp.clip(space_duals[level_idx] + SIGMA * details[level_idx], -SPACE_BOUND, SPACE_BOUND)
-            for level_idx in range(SCALES)
-        ]
-    )
-    space_term = synthesise(space_next)
+    space_term, space_next = spatial(image_cube, space_duals)
     spectral_sum, freq_next = spectral(pixel_cube, freq_duals)
     returned = lax.all_to_all(
         spectral_sum.reshape(chans * peers, 1, share),

time: 262 us -> 1000 us (3.82)
  the two profiles are of different devices: /device:TPU:0 before, /device:TPU:13 now
where the time goes in v3:
time: 1000 us; the launch traced here: 995 us
  Pallas kernels  789 us (79%)
  waiting for transfers between devices  75.2 us (8%)
  local copies, waits for them, and re-layouts  55.8 us (6%)
  matrix products  26.1 us (3%)
  other arithmetic  25.5 us (3%)
  starting transfers between devices  21.6 us (2%)
    pallas_call x1, Pallas kernels, starlet(): pl.pallas_call(starlet_kernel, grid=(chans // block,), in_specs=[pl.Block...  789 us
    unnamed x18, local copies, waits for them, and re-layouts  35.7 us
    ppermute x1, waiting for transfers between devices, spatial(): below = lax.ppermute(own[:halo], 'rows', up)  32.5 us
  transfers between devices with their start and end apart: 6, of which 4 were waited for; matrix products, arithmetic and copies ran while one was open for 10% of the time, Pallas kernels for 79%

profile of v3, /device:TPU:13, one launch (start us, length us, event | category | flops | bytes accessed | tf_op | source)
XLA Modules:
  0.0 994.5 jit_solution(3885714061564288776)
XLA Ops:
  0.6 3.0 copy.52
  3.6 0.0 copy-start.2
  3.6 6.7 all-to-all-start
  10.3 0.0 copy-done.2
  10.3 1.2 copy.68
  11.5 0.0 copy-start.1
  11.5 0.0 copy-start.4
  11.5 2.4 fusion.24
  13.9 0.3 copy-done.1
  14.3 4.4 collective-permute-start
  18.7 0.0 copy-done.4
  18.7 1.8 copy.54
  20.5 1.1 fusion.22
  21.6 2.1 fusion.17
  23.7 7.7 broadcast_multiply_fusion
  31.4 7.2 bitcast_multiply_fusion
  38.6 19.2 %all-to-all-done = f32[128,16,256]{0,2,1:T(8,128)} async-done(((f32[128,16,256]{0,2,1:T(8,128)}), f32[128,16,256]{0,2,1:T(8,128)}, u32[]{:S(2)}, u32[]{:S(2)}) %all-to-all-start) | async-done | bytes 2097184 | tf_op jit(solution)/shard_map/all_to_all | solution.py:269
  57.8 2.9 copy.53
  60.7 0.0 copy-start
  60.7 18.6 %fusion.2 = f32[256,2048]{0,1:T(8,128)S(1)} fusion(f32[256,2048]{0,1:T(8,128)} %copy.54, f32[2048,2048]{0,1:T(8,128)} %bitcast.42, f32[2048,256]{1,0:T(8,128)} %bitcast.50), kind=kOutput, calls=%fused_computation.8 | convolution fusion | flops 6444023808 | bytes 23068672 | tf_op jit(solution)/shard_map/dot_general | solution.py:122
  79.3 0.0 copy-done
  79.3 7.5 convolution_bitcast_fusion
  86.8 10.0 %copy.55 = f32[2048,1,256]{2,1,0:T(1,128)} copy(f32[2048,1,256]{2,0,1:T(8,128)S(1)} %convolution_bitcast_fusion) | data formatting | bytes 4194304 | tf_op jit(solution)/shard_map/reshape | solution.py:275
  96.8 4.9 all-to-all-start.1
  101.7 1.5 collective-permute-start.1
  103.2 11.6 %copy.67 = f32[4,128,32,128]{3,1,2,0:T(8,128)} copy(f32[4,128,32,128]{3,2,1,0:T(8,128)} %param.6) | data formatting | bytes 16777216 | tf_op args[2]
  114.8 0.6 pad_add_fusion.first_ref
  115.5 0.0 collective-permute-done.above_ref
  115.5 32.5 %collective-permute-done.1.below_ref = f32[30,128,128]{2,1,0:T(8,128)} collective-permute-done((f32[30,128,128]{2,1,0:T(8,128)}, f32[30,128,128]{2,1,0:T(8,128)}, u32[]{:S(2)}, u32[]{:S(2)}) %collective-permute-start.1) | collective-permute-done | bytes 1966112 | tf_op jit(solution)/shard_map/ppermute | solution.py:250
  147.9 789.3 %shard_map.67 = (f32[4,32,128,128]{3,2,1,0:T(8,128)}, f32[30,128,128]{2,1,0:T(8,128)}, f32[32,128,128]{2,1,0:T(8,128)}, f32[30,128,128]{2,1,0:T(8,128)}) custom-call(s32[2]{0:T(128)} %pad_add_fusion.first_ref, f32[30,128,128]{2,1,0:T(8,128)} %collective-permute-done.above_ref, f32[32,128,128]{2,1,0:T(8,128)} %bitcast.45, ...), custom_call_target="tpu_custom_call" | custom-call | tf_op jit(solution)/shard_map/pallas_call | solution.py:224
  937.2 2.6 collective-permute-start.2
  939.8 1.5 collective-permute-start.3
  941.3 11.6 %copy.60 = f32[4,128,32,128]{3,2,1,0:T(8,128)} copy(f32[4,128,32,128]{3,1,2,0:T(8,128)} %bitcast.46) | data formatting | bytes 16777216
  953.0 1.8 copy.61
  954.8 0.0 all-to-all-done.1
  954.8 1.7 copy.62
  956.5 1.8 copy.56
  958.3 0.0 copy-start.3
  958.3 3.1 copy.57
  961.4 18.5 %collective-permute-done.2 = f32[30,128,128]{2,1,0:T(8,128)} collective-permute-done((f32[30,128,128]{2,1,0:T(8,128)}, f32[30,128,128]{2,1,0:T(8,128)}, u32[]{:S(2)}, u32[]{:S(2)}) %collective-permute-start.2) | collective-permute-done | bytes 1966112 | tf_op jit(solution)/shard_map/ppermute | solution.py:253
  979.9 5.1 collective-permute-done.3
  985.0 0.0 copy-done.3
  985.0 6.8 fusion.6
  991.7 2.5 copy.59
  (3 shorter events, 0.0 us)
Async XLA Ops:
  3.6 6.7 copy-start.2
  3.6 54.2 %all-to-all-start = ((f32[128,16,256]{0,2,1:T(8,128)}), f32[128,16,256]{0,2,1:T(8,128)}, u32[]{:S(2)}, u32[]{:S(2)}) async-start(f32[128,16,256]{0,2,1:T(8,128)} %bitcast.47), calls=%async_computation | async-start | bytes 4194304 | tf_op jit(solution)/shard_map/all_to_all | solution.py:269
  11.5 2.8 copy-start.1
  11.5 7.1 copy-start.4
  14.3 101.2 %collective-permute-start = (f32[30,128,128]{2,1,0:T(8,128)}, f32[30,128,128]{2,1,0:T(8,128)}, u32[]{:S(2)}, u32[]{:S(2)}) collective-permute-start(f32[30,128,128]{2,1,0:T(8,128)} %get-tuple-element.27), channel_id=1, source_target_pairs={{0,1},{2,3},{4,5},{6,7},{8,9},{10,11},{12,13},{14,15},{16,17},{18,... | collective-permute-start | bytes 5898248 | tf_op jit(solution)/shard_map/ppermute | solution.py:249
  60.7 18.6 %copy-start = (f32[2048,2048]{0,1:T(8,128)S(1)}, f32[2048,2048]{0,1:T(8,128)}, u32[]{:S(2)}) copy-start(f32[2048,2048]{0,1:T(8,128)} %bitcast_multiply_fusion) | copy-start | bytes 50331652
  96.8 858.0 %all-to-all-start.1 = ((f32[2048,1,256]{2,1,0:T(1,128)}), f32[2048,1,256]{2,1,0:T(1,128)}, u32[]{:S(2)}, u32[]{:S(2)}) async-start(f32[2048,1,256]{2,1,0:T(1,128)} %copy.55), calls=%async_computation.1 | async-start | bytes 4194304 | tf_op jit(solution)/shard_map/all_to_all | solution.py:274
  101.7 46.2 %collective-permute-start.1 = (f32[30,128,128]{2,1,0:T(8,128)}, f32[30,128,128]{2,1,0:T(8,128)}, u32[]{:S(2)}, u32[]{:S(2)}) collective-permute-start(f32[30,128,128]{2,1,0:T(8,128)} %get-tuple-element.26), channel_id=1, source_target_pairs={{1,0},{3,2},{5,4},{7,6},{9,8},{11,10},{13,12},{15,14},{17,16},{19,... | collective-permute-start | bytes 5898248 | tf_op jit(solution)/shard_map/ppermute | solution.py:250
  937.2 42.6 %collective-permute-start.2 = (f32[30,128,128]{2,1,0:T(8,128)}, f32[30,128,128]{2,1,0:T(8,128)}, u32[]{:S(2)}, u32[]{:S(2)}) collective-permute-start(f32[30,128,128]{2,1,0:T(8,128)} %get-tuple-element.8), channel_id=1, source_target_pairs={{0,1},{2,3},{4,5},{6,7},{8,9},{10,11},{12,13},{14,15},{16,17},{18,... | collective-permute-start | bytes 5898248 | tf_op jit(solution)/shard_map/ppermute | solution.py:253
  939.8 45.2 %collective-permute-start.3 = (f32[30,128,128]{2,1,0:T(8,128)}, f32[30,128,128]{2,1,0:T(8,128)}, u32[]{:S(2)}, u32[]{:S(2)}) collective-permute-start(f32[30,128,128]{2,1,0:T(8,128)} %get-tuple-element.9), channel_id=1, source_target_pairs={{1,0},{3,2},{5,4},{7,6},{9,8},{11,10},{13,12},{15,14},{17,16},{19,... | collective-permute-start | bytes 5898248 | tf_op jit(solution)/shard_map/ppermute | solution.py:254
  958.3 26.6 %copy-start.3 = (f32[128,32,128]{2,1,0:T(8,128)S(1)}, f32[128,32,128]{2,1,0:T(8,128)}, u32[]{:S(2)}) copy-start(f32[128,32,128]{2,1,0:T(8,128)} %param.4) | copy-start | bytes 6291460
